TPU v7x, 256 devices: a whole 4x4x8 slice. The times are simulated.
256 devices in a mesh: dp: 4 (over y), tp: 64 (over x, z, core).
Axes of the slice: x: 4, y: 4, z: 8, core: 2. Of those that a mesh axis runs over, the one named last changes fastest.
Arguments:
- attn_heads: bfloat16 [4, 8192, 2048], P(None, 'tp', 'dp'), may hold values from -1.5 to 1.5
- w_out: bfloat16 [2048, 2048], P('dp'), may hold values from -0.125 to 0.125
- residual: bfloat16 [32768, 2048], P(('dp', 'tp')), may hold values from -1.5 to 1.5
- moe_gain: float32 [2048], replicated, may hold values from 0.1 to 1.9
- router: bfloat16 [2048, 64], replicated, may hold values from -0.0625 to 0.0625
- expert_ids: int32 [32768, 8], P(('dp', 'tp')), may hold values from 0 to 63, all different within a row; in each aligned block of 128 rows (0 to 127, 128 to 255, ...) at most 24 rows name the same one
- w_gate_up: bfloat16 [64, 2048, 1024], P('tp'), may hold values from -0.125 to 0.125
- w_down: bfloat16 [64, 512, 2048], P('tp'), may hold values from -0.75 to 0.75
- next_gain: float32 [2048], replicated, may hold values from 0.1 to 1.9
Outputs:
- layer_out: bfloat16 [32768, 2048], P(('dp', 'tp'))
- next_input: bfloat16 [4, 8192, 2048], P(None, 'tp')
Inputs may be any that keep to these rules, and one draw needn't show every extreme that they name: `expert_ids`: each row names 8 different experts. In each aligned block of 128 rows (the rows of one device) no expert is named by more than 24 rows, a bound that some block reaches.
All inputs are finite; a program needn't handle non-finite values.
Results may differ from a plain program's by a relative error of at most 0.0095.
Values may be sent and summed in bfloat16 or wider, within the bound.
No kernel may reach another device: no remote copies, remote signals or barrier semaphores. Data moves between devices by JAX's collectives and lax.ppermute only.
A program may use at most 128 MiB of HBM per device.

v0:
```python
import jax
import jax.numpy as jnp
from jax import lax
from jax.sharding import PartitionSpec as P

EPS = 1e-05


def rms_scale(values, gain_vector):
    mean_square = jnp.mean(values * values, axis=-1, keepdims=True)
    return values * lax.rsqrt(mean_square + EPS) * gain_vector


def expert_block(row_block, gate_up, down_proj):
    hidden_width = down_proj.shape[0]
    projected_up = jnp.dot(row_block, gate_up, preferred_element_type=jnp.float32)
    activated = (
        jax.nn.silu(projected_up[:, :hidden_width]) * projected_up[:, hidden_width:]
    ).astype(jnp.bfloat16)
    return jnp.dot(activated, down_proj, preferred_element_type=jnp.float32).astype(jnp.bfloat16)


def local(attn_heads, w_out, residual, moe_gain, router, expert_ids, w_gate_up, w_down, next_gain):
    groups, tok_rows, quarter = attn_heads.shape
    feat_width = w_out.shape[1]
    flat_heads = attn_heads.reshape(groups * tok_rows, quarter)
    projected = lax.psum_scatter(
        jnp.dot(flat_heads, w_out, preferred_element_type=jnp.float32),
        "dp",
        scatter_dimension=0,
        tiled=True,
    )
    mid_state = (residual.astype(jnp.float32) + projected).astype(jnp.bfloat16)
    mid_wide = mid_state.astype(jnp.float32)
    normed = rms_scale(mid_wide, moe_gain).astype(jnp.bfloat16)
    logits = jnp.dot(normed, router, preferred_element_type=jnp.float32)
    experts = router.shape[1]
    top_count = expert_ids.shape[1]
    capacity = min(tok_rows, 3 * tok_rows * top_count // (2 * experts))
    expert_pos = jnp.arange(experts, dtype=jnp.int32)
    chosen = expert_ids[:, :, None] == expert_pos[None, None, :]
    picked = jnp.sum(jnp.where(chosen, logits[:, None, :], 0.0), axis=2)
    raised = jnp.exp(picked)
    gate_weights = raised / jnp.sum(raised, axis=1, keepdims=True)
    member = jnp.sum(chosen.astype(jnp.float32), axis=1)
    row_pos = jnp.arange(tok_rows, dtype=jnp.int32)
    earlier = (row_pos[None, :] < row_pos[:, None]).astype(jnp.bfloat16)
    row_ranks = jnp.dot(
        earlier, member.astype(jnp.bfloat16), preferred_element_type=jnp.float32
    ).astype(jnp.int32)
    slot_pos = jnp.arange(capacity, dtype=jnp.int32)
    placed = (member.T[:, None, :] > 0) & (row_ranks.T[:, None, :] == slot_pos[None, :, None])
    source_row = jnp.sum(jnp.where(placed, row_pos[None, None, :], 0), axis=2, dtype=jnp.int32)
    filled = jnp.any(placed, axis=2)
    taken = jnp.take(normed, source_row.reshape(-1), axis=0).reshape(experts, capacity, feat_width)
    outgoing = jnp.where(filled[:, :, None], taken, jnp.zeros((), jnp.bfloat16))
    slot_of = jnp.sum(jnp.where(chosen, row_ranks[:, None, :], 0), axis=2, dtype=jnp.int32)
    gate_up = w_gate_up[0]
    down_proj = w_down[0]
    arrived = lax.all_to_all(outgoing, "tp", split_axis=0, concat_axis=0, tiled=True)
    served = expert_block(arrived.reshape(-1, feat_width), gate_up, down_proj).reshape(
        arrived.shape
    )
    returned = lax.all_to_all(served, "tp", split_axis=0, concat_axis=0, tiled=True)
    flat_back = returned.reshape(experts * capacity, feat_width)
    pick_index = (expert_ids * capacity + slot_of).reshape(-1)
    fetched = jnp.take(flat_back, pick_index, axis=0).reshape(tok_rows, top_count, feat_width)
    expert_sum = jnp.zeros((tok_rows, feat_width), jnp.float32)
    for slot_choice in range(top_count):
        expert_sum = expert_sum + gate_weights[:, slot_choice : slot_choice + 1] * fetched[
            :, slot_choice, :
        ].astype(jnp.float32)
    layer_sum = mid_wide + expert_sum
    layer_out = layer_sum.astype(jnp.bfloat16)
    next_local = rms_scale(layer_sum, next_gain).astype(jnp.bfloat16)
    next_input = lax.all_gather(next_local[None], "dp", axis=0, tiled=True)
    return (layer_out, next_input)


def solution(mesh):
    in_specs = (
        P(None, "tp", "dp"),
        P("dp", None),
        P(("dp", "tp"), None),
        P(),
        P(),
        P(("dp", "tp"), None),
        P("tp", None, None),
        P("tp", None, None),
        P(),
    )
    out_specs = (P(("dp", "tp"), None), P(None, "tp", None))
    return jax.shard_map(local, mesh=mesh, in_specs=in_specs, out_specs=out_specs, check_vma=False)
```

profile of v0, /device:TPU:1, one launch (start us, length us, event | category | flops | bytes accessed | tf_op | source)
XLA Modules:
  0.0 453.9 jit_solution(17140186375868702840)
XLA Ops:
  7.2 0.0 copy-start
  7.2 0.0 reduce-scatter.2.cloned.1.call-start
  7.2 0.0 copy-start.2
  7.2 5.1 %fusion.21 = f32[512,2048]{1,0:T(8,128)} fusion(bf16[512,512]{1,0:T(8,128)(2,1)} %bitcast.93, bf16[512,2048]{1,0:T(8,128)(2,1)} %param.10), kind=kOutput, calls=%fused_computation.78 | convolution fusion | flops 1073741824 | bytes 6815744 | tf_op jit(solution)/shard_map/dot_general | solution.py:28
  12.3 0.0 copy-start.5
  12.3 0.0 copy-start.3
  12.3 0.0 copy-start.4
  12.3 0.0 reduce-scatter.2.cloned.1.call-update
  12.4 53.3 %reduce-scatter.2.cloned.1.call-done = f32[128,2048]{1,0:T(8,128)} async-done(((f32[512,2048]{1,0:T(8,128)}), f32[128,2048]{1,0:T(8,128)}) %reduce-scatter.2.cloned.1.call-update) | async-done | bytes 1048592 | tf_op jit(solution)/shard_map/reduce_scatter | solution.py:27
  65.6 0.0 copy-done.2
  65.6 1.5 fusion.6
  67.1 0.0 copy-done.5
  67.1 0.2 fusion.8
  67.3 0.0 copy-done.3
  67.3 0.3 fusion.22
  67.6 0.0 copy-done.4
  67.7 0.1 select_reduce_fusion.2
  67.7 0.1 convolution_convert_fusion.1
  67.9 1.2 fusion.17
  69.1 1.2 select_reduce_fusion
  70.2 0.1 reshape.145
  70.4 7.1 %gather_fusion = bf16[1536,2048]{1,0:T(8,128)(2,1)} fusion(bf16[128,2048]{1,0:T(8,128)(2,1)S(1)} %fusion.8, s32[2048]{0:T(1024)S(1)} %pad_clamp_fusion), kind=kCustom, calls=%fused_computation | custom fusion | bytes 12589056 | tf_op jit(solution)/shard_map/jit(_take)/gather | solution.py:55
  77.5 3.9 select_select_fusion
  81.4 0.0 copy-start.7
  81.4 151.9 %all_to_all.10 = bf16[64,24,2048]{2,1,0:T(8,128)(2,1)S(1)} all-to-all(bf16[64,24,2048]{2,1,0:T(8,128)(2,1)S(1)} %select_select_fusion), channel_id=1, replica_groups=mesh['dp'=4,'tp'=64] {'tp'}, dimensions={0} | all-to-all | bytes 12582912 | tf_op jit(solution)/shard_map/all_to_all | solution.py:60
  233.3 0.0 copy-done.7
  233.3 6.7 %fusion = f32[1536,1024]{1,0:T(8,128)S(1)} fusion(bf16[1536,2048]{1,0:T(8,128)(2,1)S(1)} %bitcast.89, bf16[1,2048,1024]{2,1,0:T(8,128)(2,1)S(1)} %copy-done.7), kind=kOutput, calls=%fused_computation.4 | convolution fusion | flops 6442450944 | bytes 16777216 | tf_op jit(solution)/shard_map/dot_general | solution.py:16
  240.0 0.0 copy-done
  240.0 5.3 %convolution_convert_fusion = bf16[1536,2048]{1,0:T(8,128)(2,1)} fusion(bf16[1,512,2048]{2,1,0:T(8,128)(2,1)S(1)} %copy-done, f32[1536,1024]{1,0:T(8,128)S(1)} %fusion), kind=kOutput, calls=%fused_computation.2 | convolution fusion | flops 3229089792 | bytes 14680064 | tf_op jit(solution)/shard_map/dot_general | solution.py:20
  245.4 6.0 %all-to-all-start.1 = ((bf16[64,24,2048]{2,1,0:T(8,128)(2,1)}), bf16[64,24,2048]{2,1,0:T(8,128)(2,1)}, u32[]{:S(2)}, u32[]{:S(2)}) async-start(bf16[64,24,2048]{2,1,0:T(8,128)(2,1)} %bitcast.88), calls=%async_computation.2 | async-start | bytes 12582912 | tf_op jit(solution)/shard_map/all_to_all | solution.py:64
  251.4 0.3 all-gather.3.cloned.1.call-start
  251.7 0.1 copy.21
  251.8 0.1 reshape.149
  252.0 140.2 %all-to-all-done.1 = bf16[64,24,2048]{2,1,0:T(8,128)(2,1)} async-done(((bf16[64,24,2048]{2,1,0:T(8,128)(2,1)}), bf16[64,24,2048]{2,1,0:T(8,128)(2,1)}, u32[]{:S(2)}, u32[]{:S(2)}) %all-to-all-start.1) | async-done | bytes 6291488 | tf_op jit(solution)/shard_map/all_to_all | solution.py:64
  392.2 12.4 %gather_fusion.1 = bf16[1024,2048]{1,0:T(8,128)(2,1)} fusion(bf16[1536,2048]{1,0:T(8,128)(2,1)} %bitcast.9, s32[1024]{0:T(1024)S(1)} %broadcast_clamp_fusion), kind=kCustom, calls=%fused_computation.1 | custom fusion | bytes 8392704 | tf_op jit(solution)/shard_map/jit(_take)/gather | solution.py:67
  404.6 8.8 %copy_select_fusion = bf16[128,8,2048]{2,0,1:T(8,128)(2,1)S(1)} fusion(bf16[128,8,2048]{2,1,0:T(8,128)(2,1)} %bitcast.87, pred[128,8]{0,1:T(8,128)(4,1)S(1)} %get-tuple-element.6), kind=kLoop, calls=%fused_computation.6 | loop fusion | flops 2097152 | bytes 8389632 | tf_op jit(solution)/shard_map/jit(_take)/select_n | solution.py:67
  413.4 0.0 copy-start.6
  413.4 0.0 copy-start.1
  413.4 1.1 multiply_reduce_fusion
  414.5 0.0 copy-done.6
  414.5 1.1 multiply_convert_fusion
  415.7 0.0 all-gather.3.cloned.1.call-update
  415.7 28.3 %all-gather.3.cloned.1.call-done = bf16[512,2048]{1,0:T(8,128)(2,1)} async-done(((bf16[128,2048]{1,0:T(8,128)(2,1)}), bf16[512,2048]{1,0:T(8,128)(2,1)}) %all-gather.3.cloned.1.call-update) | async-done | bytes 2097168 | tf_op jit(solution)/shard_map/all_gather | solution.py:76
  443.9 3.2 copy.25
  447.1 0.0 copy-done.1
  (13 shorter events, 0.2 us)
Async XLA Ops:
  7.2 232.9 %copy-start = (bf16[1,512,2048]{2,1,0:T(8,128)(2,1)S(1)}, bf16[1,512,2048]{2,1,0:T(8,128)(2,1)}, u32[]{:S(2)}) copy-start(bf16[1,512,2048]{2,1,0:T(8,128)(2,1)} %param.16) | copy-start | bytes 6291460
  7.2 58.5 %reduce-scatter.2.cloned.1.call-start = ((), (), s32[]{:S(2)}) async-start(), calls=%async_computation.3 | async-start | bytes 5242880 | tf_op jit(solution)/shard_map/reduce_scatter | solution.py:27
  7.2 58.4 %copy-start.2 = (bf16[128,2048]{1,0:T(8,128)(2,1)S(1)}, bf16[128,2048]{1,0:T(8,128)(2,1)}, u32[]{:S(2)}) copy-start(bf16[128,2048]{1,0:T(8,128)(2,1)} %param.11) | copy-start | bytes 1572868
  12.3 54.8 %copy-start.5 = (f32[2048]{0:T(1024)S(1)}, f32[2048]{0:T(1024)}, u32[]{:S(2)}) copy-start(f32[2048]{0:T(1024)} %param.12) | copy-start | bytes 24580
  12.3 55.0 %copy-start.3 = (bf16[2048,64]{0,1:T(8,128)(2,1)S(1)}, bf16[2048,64]{0,1:T(8,128)(2,1)}, u32[]{:S(2)}) copy-start(bf16[2048,64]{0,1:T(8,128)(2,1)} %param.13) | copy-start | bytes 786436
  12.3 55.3 %copy-start.4 = (s32[128,8]{0,1:T(8,128)S(1)}, s32[128,8]{0,1:T(8,128)}, u32[]{:S(2)}) copy-start(s32[128,8]{0,1:T(8,128)} %param.14) | copy-start | bytes 12292
  81.4 151.9 %copy-start.7 = (bf16[1,2048,1024]{2,1,0:T(8,128)(2,1)S(1)}, bf16[1,2048,1024]{2,1,0:T(8,128)(2,1)}, u32[]{:S(2)}) copy-start(bf16[1,2048,1024]{2,1,0:T(8,128)(2,1)} %param.15) | copy-start | bytes 12582916
  245.4 146.8 %all-to-all-start.1 = ((bf16[64,24,2048]{2,1,0:T(8,128)(2,1)}), bf16[64,24,2048]{2,1,0:T(8,128)(2,1)}, u32[]{:S(2)}, u32[]{:S(2)}) async-start(bf16[64,24,2048]{2,1,0:T(8,128)(2,1)} %bitcast.88), calls=%async_computation.2 | async-start | bytes 12582912 | tf_op jit(solution)/shard_map/all_to_all | solution.py:64
  251.4 192.6 %all-gather.3.cloned.1.call-start = ((), (), s32[]{:S(2)}) async-start(), calls=%async_computation.4 | async-start | bytes 2621440 | tf_op jit(solution)/shard_map/all_gather | solution.py:76
  413.4 1.1 copy-start.6
  413.4 33.7 %copy-start.1 = (bf16[1,512,2048]{2,1,0:T(8,128)(2,1)S(1)}, bf16[1,512,2048]{2,1,0:T(8,128)(2,1)}, u32[]{:S(2)}) copy-start(bf16[1,512,2048]{2,1,0:T(8,128)(2,1)} %param.16) | copy-start | bytes 6291460
Sparse Core Ops, SparseCore 0:
  12.5 53.1 reduce-scatter.1
  415.8 28.0 all-gather.2
where the time goes:
time: 454 us
  waiting for transfers between devices  222 us (49%)
  blocking collectives  152 us (33%)
  local copies, waits for them, and re-layouts  23 us (5%)
  other arithmetic  19.2 us (4%)
  matrix products  17.5 us (4%)
  between operations  14.2 us (3%)
  starting transfers between devices  6.3 us (1%)
    all_to_all x1, blocking collectives, local(): lax.all_to_all(outgoing, 'tp', split_axis=0, concat_axis=0, tiled=True)  152 us
    all_to_all x1, waiting for transfers between devices, local(): lax.all_to_all(served, 'tp', split_axis=0, concat_axis=0, tiled=True)  140 us
    reduce_scatter x1, waiting for transfers between devices, local(): lax.psum_scatter(jnp.dot(flat_heads, w_out, preferred_element_type=jnp.fl...  53.3 us
    all_gather x1, waiting for transfers between devices, local(): next_input = lax.all_gather(next_local[None], 'dp', axis=0, tiled=True)  28.3 us
    gather x1, local copies, waits for them, and re-layouts, local(): jnp.take(flat_back, pick_index, axis=0)  12.4 us
  transfers between devices with their start and end apart: 3, of which 3 were waited for; matrix products, arithmetic and copies ran while one was open for 0% of the time, Pallas kernels for 0%

commit v1 on v0

v1 whole, which is shorter than its diff:
```python
import jax
import jax.numpy as jnp
from jax import lax
from jax.sharding import PartitionSpec as P

EPS = 1e-05
CHUNKS = 4


def rms_scale(values, gain_vector):
    mean_square = jnp.mean(values * values, axis=-1, keepdims=True)
    return values * lax.rsqrt(mean_square + EPS) * gain_vector


def split_hi_lo(values):
    high = values.astype(jnp.bfloat16)
    low = (values - high.astype(jnp.float32)).astype(jnp.bfloat16)
    return high, low


def local(attn_heads, w_out, residual, moe_gain, router, expert_ids, w_gate_up, w_down, next_gain):
    groups, tok_rows, quarter = attn_heads.shape
    feat_width = w_out.shape[1]
    experts = router.shape[1]
    top_count = expert_ids.shape[1]
    capacity = min(tok_rows, 3 * tok_rows * top_count // (2 * experts))
    slots = experts * capacity
    step = feat_width // CHUNKS

    expert_pos = jnp.arange(experts, dtype=jnp.int32)
    chosen = expert_ids[:, :, None] == expert_pos[None, None, :]
    member = jnp.sum(chosen.astype(jnp.float32), axis=1)
    row_pos = jnp.arange(tok_rows, dtype=jnp.int32)
    earlier = (row_pos[None, :] < row_pos[:, None]).astype(jnp.bfloat16)
    row_ranks = jnp.dot(
        earlier, member.astype(jnp.bfloat16), preferred_element_type=jnp.float32
    ).astype(jnp.int32)
    slot_pos = jnp.arange(capacity, dtype=jnp.int32)
    placed = (member.T[:, None, :] > 0) & (row_ranks.T[:, None, :] == slot_pos[None, :, None])
    dispatch = placed.reshape(slots, tok_rows).astype(jnp.bfloat16)

    flat_heads = attn_heads.reshape(groups * tok_rows, quarter)
    partials = [
        jnp.dot(flat_heads, w_out[:, c * step : (c + 1) * step], preferred_element_type=jnp.float32)
        for c in range(CHUNKS)
    ]
    part = lax.psum_scatter(partials[0], "dp", scatter_dimension=0, tiled=True)
    mid_parts = []
    arrived_parts = []
    for c in range(CHUNKS):
        cols = slice(c * step, (c + 1) * step)
        res_c, part = lax.optimization_barrier((residual[:, cols], part))
        mid_c = (res_c.astype(jnp.float32) + part).astype(jnp.bfloat16)
        mid_parts.append(mid_c)
        outgoing = jnp.dot(dispatch, mid_c, preferred_element_type=jnp.float32).astype(jnp.bfloat16)
        if c + 1 < CHUNKS:
            outgoing, following = lax.optimization_barrier((outgoing, partials[c + 1]))
            part = lax.psum_scatter(following, "dp", scatter_dimension=0, tiled=True)
        arrived_parts.append(
            lax.all_to_all(
                outgoing.reshape(experts, capacity, step), "tp", split_axis=0, concat_axis=0, tiled=True
            ).reshape(slots, step)
        )

    mid_state = jnp.concatenate(mid_parts, axis=1)
    mid_wide = mid_state.astype(jnp.float32)
    normed = rms_scale(mid_wide, moe_gain).astype(jnp.bfloat16)
    logits = jnp.dot(normed, router, preferred_element_type=jnp.float32)
    picked = jnp.sum(jnp.where(chosen, logits[:, None, :], 0.0), axis=2)
    raised = jnp.exp(picked)
    gate_weights = raised / jnp.sum(raised, axis=1, keepdims=True)
    weight_full = jnp.sum(jnp.where(chosen, gate_weights[:, :, None], 0.0), axis=1)
    combine = jnp.where(placed, weight_full.T[:, None, :], 0.0).reshape(slots, tok_rows)
    combine_hi, combine_lo = split_hi_lo(combine)

    arrived = jnp.concatenate(arrived_parts, axis=1).astype(jnp.float32)
    arrived_normed = rms_scale(arrived, moe_gain).astype(jnp.bfloat16)
    gate_up = w_gate_up[0]
    down_proj = w_down[0]
    hidden_width = down_proj.shape[0]
    projected_up = jnp.dot(arrived_normed, gate_up, preferred_element_type=jnp.float32)
    activated = (
        jax.nn.silu(projected_up[:, :hidden_width]) * projected_up[:, hidden_width:]
    ).astype(jnp.bfloat16)

    sum_parts = []
    for c in range(CHUNKS):
        cols = slice(c * step, (c + 1) * step)
        served = jnp.dot(activated, down_proj[:, cols], preferred_element_type=jnp.float32).astype(
            jnp.bfloat16
        )
        returned = lax.all_to_all(
            served.reshape(experts, capacity, step), "tp", split_axis=0, concat_axis=0, tiled=True
        ).reshape(slots, step)
        dims = (((0,), (0,)), ((), ()))
        expert_sum = lax.dot_general(
            combine_hi, returned, dims, preferred_element_type=jnp.float32
        ) + lax.dot_general(combine_lo, returned, dims, preferred_element_type=jnp.float32)
        sum_parts.append(mid_wide[:, cols] + expert_sum)

    layer_sum = jnp.concatenate(sum_parts, axis=1)
    layer_out = layer_sum.astype(jnp.bfloat16)
    next_local = rms_scale(layer_sum, next_gain).astype(jnp.bfloat16)
    next_input = lax.all_gather(next_local[None], "dp", axis=0, tiled=True)
    return (layer_out, next_input)


def solution(mesh):
    in_specs = (
        P(None, "tp", "dp"),
        P("dp", None),
        P(("dp", "tp"), None),
        P(),
        P(),
        P(("dp", "tp"), None),
        P("tp", None, None),
        P("tp", None, None),
        P(),
    )
    out_specs = (P(("dp", "tp"), None), P(None, "tp", None))
    return jax.shard_map(local, mesh=mesh, in_specs=in_specs, out_specs=out_specs, check_vma=False)
```

time: 454 us -> 477 us (1.051)
  blocking collectives: 152 us -> 45.9 us
  waiting for transfers between devices: 222 us -> 297 us
  starting transfers between devices: 6.3 us -> 49.9 us
  matrix products: 17.5 us -> 52.3 us
  local copies, waits for them, and re-layouts: 23 us -> 4.94 us
  other arithmetic: 19.2 us -> 12.1 us
    all_to_all x1, blocking collectives: 152 us -> 45.9 us  [local(): lax.all_to_all(outgoing.reshape(experts, capacity, step), 'tp', split_axi...]
    reduce_scatter x1 -> x4, waiting for transfers between devices: 53.3 us -> 101 us  [the longest x3 76.3 us: local(): part = lax.psum_scatter(following, 'dp', scatter_dimension=0, tiled=True)]
    all_to_all x1 -> x7, starting transfers between devices: 6 us -> 49.7 us  [the longest x4 25.1 us: local(): lax.all_to_all(served.reshape(experts, capacity, step), 'tp', split_axis=...]
    dot_general x3 -> x21, matrix products: 17.1 us -> 51.8 us  [the longest x4 14.5 us: local(): jnp.dot(activated, down_proj[:, cols], preferred_element_type=jnp.float32)]
    all_to_all x1 -> x7, waiting for transfers between devices: 140 us -> 166 us  [the longest x4 138 us: local(): lax.all_to_all(served.reshape(experts, capacity, step), 'tp', split_axis=...]
    gather x2 -> x0, local copies, waits for them, and re-layouts: 19.5 us -> none  [the longest x1 12.4 us: local(): jnp.take(flat_back, pick_index, axis=0)]
    select_n x4 -> x0, other arithmetic: 12.8 us -> none  [the longest x2 8.83 us: local(): jnp.take(flat_back, pick_index, axis=0)]
    convert_element_type x1 -> x7, other arithmetic: 0.19 us -> 6.78 us  [the longest x4 3.9 us: local(): mid_c = (res_c.astype(jnp.float32) + part).astype(jnp.bfloat16)]
  transfers between devices with their start and end apart: 3 -> 12, of which waited for: 3 -> 12; matrix products, arithmetic and copies ran while one was open for 0% -> 8% of each run, Pallas kernels for 0% -> 0%
where the time goes in v1:
time: 477 us; the launch traced here: 476 us
  waiting for transfers between devices  297 us (62%)
  matrix products  52.3 us (11%)
  starting transfers between devices  49.9 us (10%)
  blocking collectives  45.9 us (10%)
  between operations  14.2 us (3%)
  other arithmetic  12.1 us (3%)
  local copies, waits for them, and re-layouts  4.94 us (1%)
    all_to_all x4, waiting for transfers between devices, local(): lax.all_to_all(served.reshape(experts, capacity, step), 'tp', split_axis=...  138 us
    reduce_scatter x3, waiting for transfers between devices, local(): part = lax.psum_scatter(following, 'dp', scatter_dimension=0, tiled=True)  76.3 us
    all_to_all x1, blocking collectives, local(): lax.all_to_all(outgoing.reshape(experts, capacity, step), 'tp', split_axi...  45.9 us
    all_to_all x3, waiting for transfers between devices, local(): lax.all_to_all(outgoing.reshape(experts, capacity, step), 'tp', split_axi...  27.8 us
    all_gather x1, waiting for transfers between devices, local(): next_input = lax.all_gather(next_local[None], 'dp', axis=0, tiled=True)  27.7 us
    reduce_scatter x1, waiting for transfers between devices, local(): part = lax.psum_scatter(partials[0], 'dp', scatter_dimension=0, tiled=True)  25.1 us
    all_to_all x4, starting transfers between devices, local(): lax.all_to_all(served.reshape(experts, capacity, step), 'tp', split_axis=...  25.1 us
    all_to_all x3, starting transfers between devices, local(): lax.all_to_all(outgoing.reshape(experts, capacity, step), 'tp', split_axi...  24.7 us
  transfers between devices with their start and end apart: 12, of which 12 were waited for; matrix products, arithmetic and copies ran while one was open for 8% of the time, Pallas kernels for 0%

profile of v1, /device:TPU:1, one launch (start us, length us, event | category | flops | bytes accessed | tf_op | source)
XLA Modules:
  0.0 475.8 jit_solution(12255662636266115392)
XLA Ops:
  7.2 1.0 copy-done
  8.2 2.4 fusion.36
  11.9 2.5 fusion.34
  14.4 25.1 %reduce-scatter.5.cloned.1.call-done = f32[128,512]{1,0:T(8,128)} async-done(((f32[512,512]{1,0:T(8,128)}), f32[128,512]{1,0:T(8,128)}) %reduce-scatter.5.cloned.1.call-update) | async-done | bytes 262160 | tf_op jit(solution)/shard_map/reduce_scatter | solution.py:47
  39.5 1.0 add_convert_fusion.3
  40.4 1.7 convolution_convert_fusion.7
  42.2 12.2 %all-to-all-start = ((bf16[64,24,512]{2,1,0:T(8,128)(2,1)}), bf16[64,24,512]{2,1,0:T(8,128)(2,1)S(1)}, u32[]{:S(2)}, u32[]{:S(2)}) async-start(bf16[64,24,512]{2,1,0:T(8,128)(2,1)} %bitcast.95), calls=%async_computation.4 | async-start | bytes 3145728 | tf_op jit(solution)/shard_map/all_to_all | solution.py:60
  55.1 2.5 fusion.32
  57.5 25.0 %reduce-scatter.7.cloned.1.call-done = f32[128,512]{1,0:T(8,128)} async-done(((f32[512,512]{1,0:T(8,128)}), f32[128,512]{1,0:T(8,128)}) %reduce-scatter.7.cloned.1.call-update) | async-done | bytes 262160 | tf_op jit(solution)/shard_map/reduce_scatter | solution.py:58
  82.6 1.0 add_convert_fusion.2
  83.5 1.7 convolution_convert_fusion.6
  85.2 8.8 %all-to-all-done = bf16[64,24,512]{2,1,0:T(8,128)(2,1)S(1)} async-done(((bf16[64,24,512]{2,1,0:T(8,128)(2,1)}), bf16[64,24,512]{2,1,0:T(8,128)(2,1)S(1)}, u32[]{:S(2)}, u32[]{:S(2)}) %all-to-all-start) | async-done | bytes 1572896 | tf_op jit(solution)/shard_map/all_to_all | solution.py:60
  94.1 6.3 %all-to-all-start.1 = ((bf16[64,24,512]{2,1,0:T(8,128)(2,1)}), bf16[64,24,512]{2,1,0:T(8,128)(2,1)}, u32[]{:S(2)}, u32[]{:S(2)}) async-start(bf16[64,24,512]{2,1,0:T(8,128)(2,1)} %bitcast.93), calls=%async_computation.5 | async-start | bytes 3145728 | tf_op jit(solution)/shard_map/all_to_all | solution.py:60
  101.1 2.5 fusion.30
  103.6 24.5 %reduce-scatter.9.cloned.1.call-done = f32[128,512]{1,0:T(8,128)} async-done(((f32[512,512]{1,0:T(8,128)}), f32[128,512]{1,0:T(8,128)}) %reduce-scatter.9.cloned.1.call-update) | async-done | bytes 262160 | tf_op jit(solution)/shard_map/reduce_scatter | solution.py:58
  128.0 1.0 add_convert_fusion.1
  129.0 1.7 convolution_convert_fusion.5
  130.7 9.3 %all-to-all-done.1 = bf16[64,24,512]{2,1,0:T(8,128)(2,1)} async-done(((bf16[64,24,512]{2,1,0:T(8,128)(2,1)}), bf16[64,24,512]{2,1,0:T(8,128)(2,1)}, u32[]{:S(2)}, u32[]{:S(2)}) %all-to-all-start.1) | async-done | bytes 1572896 | tf_op jit(solution)/shard_map/all_to_all | solution.py:60
  140.1 6.3 %all-to-all-start.2 = ((bf16[64,24,512]{2,1,0:T(8,128)(2,1)}), bf16[64,24,512]{2,1,0:T(8,128)(2,1)}, u32[]{:S(2)}, u32[]{:S(2)}) async-start(bf16[64,24,512]{2,1,0:T(8,128)(2,1)} %bitcast.94), calls=%async_computation.6 | async-start | bytes 3145728 | tf_op jit(solution)/shard_map/all_to_all | solution.py:60
  146.9 26.8 %reduce-scatter.11.cloned.1.call-done = f32[128,512]{1,0:T(8,128)} async-done(((f32[512,512]{1,0:T(8,128)}), f32[128,512]{1,0:T(8,128)}) %reduce-scatter.11.cloned.1.call-update) | async-done | bytes 262160 | tf_op jit(solution)/shard_map/reduce_scatter | solution.py:58
  173.7 1.0 add_convert_fusion
  174.7 1.7 convolution_convert_fusion.4
  176.4 9.6 %all-to-all-done.2 = bf16[64,24,512]{2,1,0:T(8,128)(2,1)} async-done(((bf16[64,24,512]{2,1,0:T(8,128)(2,1)}), bf16[64,24,512]{2,1,0:T(8,128)(2,1)}, u32[]{:S(2)}, u32[]{:S(2)}) %all-to-all-start.2) | async-done | bytes 1572896 | tf_op jit(solution)/shard_map/all_to_all | solution.py:60
  186.0 45.9 %all_to_all.40 = bf16[64,24,512]{2,1,0:T(8,128)(2,1)S(1)} all-to-all(bf16[64,24,512]{2,1,0:T(8,128)(2,1)} %bitcast.98), channel_id=1, replica_groups=mesh['dp'=4,'tp'=64] {'tp'}, dimensions={0} | all-to-all | bytes 3145728 | tf_op jit(solution)/shard_map/all_to_all | solution.py:60
  231.9 3.6 fusion
  235.5 8.7 %fusion.3 = f32[1536,1024]{1,0:T(8,128)S(1)} fusion(f32[2048]{0:T(1024)S(1)} %copy-done.13, f32[1536]{0:T(1024)S(1)} %add_rsqrt_fusion, bf16[1,2048,1024]{2,1,0:T(8,128)(2,1)S(1)} %copy-done.11, bf16[1536,512]{1,0:T(8,128)(2,1)S(1)} %bitcast.97, bf16[1536,512]{1,0:T(8,128)(2,1)} %bitcast.10, bf16[1536,512]{1,0:T(8,128)(2,1)} %bitcast.8, ...), kind=kOutput, calls=%fused_computation.5 | convolution fusion | flops 6477053952 | bytes 16791552 | tf_op jit(solution)/shard_map/dot_general | solution.py:81
  244.2 1.0 fusion.8
  245.2 3.6 convolution_convert_fusion
  248.8 6.3 %all-to-all-start.7 = ((bf16[64,24,512]{2,1,0:T(8,128)(2,1)}), bf16[64,24,512]{2,1,0:T(8,128)(2,1)S(1)}, u32[]{:S(2)}, u32[]{:S(2)}) async-start(bf16[64,24,512]{2,1,0:T(8,128)(2,1)} %bitcast.106), calls=%async_computation.11 | async-start | bytes 3145728 | tf_op jit(solution)/shard_map/all_to_all | solution.py:92
  255.1 3.6 convolution_convert_fusion.1
  258.7 36.1 %all-to-all-done.7 = bf16[64,24,512]{2,1,0:T(8,128)(2,1)S(1)} async-done(((bf16[64,24,512]{2,1,0:T(8,128)(2,1)}), bf16[64,24,512]{2,1,0:T(8,128)(2,1)S(1)}, u32[]{:S(2)}, u32[]{:S(2)}) %all-to-all-start.7) | async-done | bytes 1572896 | tf_op jit(solution)/shard_map/all_to_all | solution.py:92
  294.8 6.3 %all-to-all-start.6 = ((bf16[64,24,512]{2,1,0:T(8,128)(2,1)}), bf16[64,24,512]{2,1,0:T(8,128)(2,1)}, u32[]{:S(2)}, u32[]{:S(2)}) async-start(bf16[64,24,512]{2,1,0:T(8,128)(2,1)} %bitcast.105), calls=%async_computation.10 | async-start | bytes 3145728 | tf_op jit(solution)/shard_map/all_to_all | solution.py:92
  301.1 3.6 convolution_convert_fusion.2
  304.7 36.1 %all-to-all-done.6 = bf16[64,24,512]{2,1,0:T(8,128)(2,1)} async-done(((bf16[64,24,512]{2,1,0:T(8,128)(2,1)}), bf16[64,24,512]{2,1,0:T(8,128)(2,1)}, u32[]{:S(2)}, u32[]{:S(2)}) %all-to-all-start.6) | async-done | bytes 1572896 | tf_op jit(solution)/shard_map/all_to_all | solution.py:92
  340.8 6.3 %all-to-all-start.5 = ((bf16[64,24,512]{2,1,0:T(8,128)(2,1)}), bf16[64,24,512]{2,1,0:T(8,128)(2,1)}, u32[]{:S(2)}, u32[]{:S(2)}) async-start(bf16[64,24,512]{2,1,0:T(8,128)(2,1)} %bitcast.104), calls=%async_computation.9 | async-start | bytes 3145728 | tf_op jit(solution)/shard_map/all_to_all | solution.py:92
  347.1 3.7 convolution_convert_fusion.3
  350.7 36.0 %all-to-all-done.5 = bf16[64,24,512]{2,1,0:T(8,128)(2,1)} async-done(((bf16[64,24,512]{2,1,0:T(8,128)(2,1)}), bf16[64,24,512]{2,1,0:T(8,128)(2,1)}, u32[]{:S(2)}, u32[]{:S(2)}) %all-to-all-start.5) | async-done | bytes 1572896 | tf_op jit(solution)/shard_map/all_to_all | solution.py:92
  386.8 6.3 %all-to-all-start.4 = ((bf16[64,24,512]{2,1,0:T(8,128)(2,1)}), bf16[64,24,512]{2,1,0:T(8,128)(2,1)}, u32[]{:S(2)}, u32[]{:S(2)}) async-start(bf16[64,24,512]{2,1,0:T(8,128)(2,1)} %bitcast.103), calls=%async_computation.8 | async-start | bytes 3145728 | tf_op jit(solution)/shard_map/all_to_all | solution.py:92
  393.8 1.0 maximum_convert_fusion
  395.3 1.8 convolution_bitcast_fusion.2
  397.1 1.8 convolution_bitcast_fusion.4
  399.4 1.8 fusion.14
  401.3 1.8 fusion.12
  403.1 29.6 %all-to-all-done.4 = bf16[64,24,512]{2,1,0:T(8,128)(2,1)} async-done(((bf16[64,24,512]{2,1,0:T(8,128)(2,1)}), bf16[64,24,512]{2,1,0:T(8,128)(2,1)}, u32[]{:S(2)}, u32[]{:S(2)}) %all-to-all-start.4) | async-done | bytes 1572896 | tf_op jit(solution)/shard_map/all_to_all | solution.py:92
  432.7 1.9 convolution_bitcast_fusion.6
  434.6 1.8 fusion.10
  438.5 27.7 %all-gather.2.cloned.1.call-done = bf16[4,128,2048]{2,1,0:T(8,128)(2,1)} async-done(((bf16[1,128,2048]{2,1,0:T(8,128)(2,1)}), bf16[4,128,2048]{2,1,0:T(8,128)(2,1)}) %all-gather.2.cloned.1.call-update) | async-done | bytes 2097168 | tf_op jit(solution)/shard_map/all_gather | solution.py:104
  466.2 3.2 copy.39
  (58 shorter events, 6.9 us)
Async XLA Ops:
  7.2 1.0 copy-start
  7.2 3.6 copy-start.9
  7.2 4.7 copy-start.8
  7.2 32.3 %reduce-scatter.5.cloned.1.call-start = ((), (), s32[]{:S(2)}) async-start(), calls=%async_computation.12 | async-start | bytes 1310720 | tf_op jit(solution)/shard_map/reduce_scatter | solution.py:47
  11.0 0.6 copy-start.3
  42.2 51.9 %all-to-all-start = ((bf16[64,24,512]{2,1,0:T(8,128)(2,1)}), bf16[64,24,512]{2,1,0:T(8,128)(2,1)S(1)}, u32[]{:S(2)}, u32[]{:S(2)}) async-start(bf16[64,24,512]{2,1,0:T(8,128)(2,1)} %bitcast.95), calls=%async_computation.4 | async-start | bytes 3145728 | tf_op jit(solution)/shard_map/all_to_all | solution.py:60
  54.3 28.2 %reduce-scatter.7.cloned.1.call-start = ((), (), s32[]{:S(2)}) async-start(), calls=%async_computation.13 | async-start | bytes 1310720 | tf_op jit(solution)/shard_map/reduce_scatter | solution.py:58
  94.1 46.0 %all-to-all-start.1 = ((bf16[64,24,512]{2,1,0:T(8,128)(2,1)}), bf16[64,24,512]{2,1,0:T(8,128)(2,1)}, u32[]{:S(2)}, u32[]{:S(2)}) async-start(bf16[64,24,512]{2,1,0:T(8,128)(2,1)} %bitcast.93), calls=%async_computation.5 | async-start | bytes 3145728 | tf_op jit(solution)/shard_map/all_to_all | solution.py:60
  100.4 27.7 %reduce-scatter.9.cloned.1.call-start = ((), (), s32[]{:S(2)}) async-start(), calls=%async_computation.14 | async-start | bytes 1310720 | tf_op jit(solution)/shard_map/reduce_scatter | solution.py:58
  140.1 46.0 %all-to-all-start.2 = ((bf16[64,24,512]{2,1,0:T(8,128)(2,1)}), bf16[64,24,512]{2,1,0:T(8,128)(2,1)}, u32[]{:S(2)}, u32[]{:S(2)}) async-start(bf16[64,24,512]{2,1,0:T(8,128)(2,1)} %bitcast.94), calls=%async_computation.6 | async-start | bytes 3145728 | tf_op jit(solution)/shard_map/all_to_all | solution.py:60
  146.3 27.4 %reduce-scatter.11.cloned.1.call-start = ((), (), s32[]{:S(2)}) async-start(), calls=%async_computation.15 | async-start | bytes 1310720 | tf_op jit(solution)/shard_map/reduce_scatter | solution.py:58
  174.7 218.6 %copy-start.1 = (bf16[128,512]{1,0:T(8,128)(2,1)}, bf16[128,512]{1,0:T(8,128)(2,1)S(1)}, u32[]{:S(2)}) copy-start(bf16[128,512]{1,0:T(8,128)(2,1)S(1)} %add_convert_fusion) | copy-start | bytes 393220
  231.9 3.6 copy-start.11
  231.9 3.6 copy-start.13
  245.2 3.6 copy-start.2
  248.8 46.0 %all-to-all-start.7 = ((bf16[64,24,512]{2,1,0:T(8,128)(2,1)}), bf16[64,24,512]{2,1,0:T(8,128)(2,1)S(1)}, u32[]{:S(2)}, u32[]{:S(2)}) async-start(bf16[64,24,512]{2,1,0:T(8,128)(2,1)} %bitcast.106), calls=%async_computation.11 | async-start | bytes 3145728 | tf_op jit(solution)/shard_map/all_to_all | solution.py:92
  294.8 46.0 %all-to-all-start.6 = ((bf16[64,24,512]{2,1,0:T(8,128)(2,1)}), bf16[64,24,512]{2,1,0:T(8,128)(2,1)}, u32[]{:S(2)}, u32[]{:S(2)}) async-start(bf16[64,24,512]{2,1,0:T(8,128)(2,1)} %bitcast.105), calls=%async_computation.10 | async-start | bytes 3145728 | tf_op jit(solution)/shard_map/all_to_all | solution.py:92
  340.8 46.0 %all-to-all-start.5 = ((bf16[64,24,512]{2,1,0:T(8,128)(2,1)}), bf16[64,24,512]{2,1,0:T(8,128)(2,1)}, u32[]{:S(2)}, u32[]{:S(2)}) async-start(bf16[64,24,512]{2,1,0:T(8,128)(2,1)} %bitcast.104), calls=%async_computation.9 | async-start | bytes 3145728 | tf_op jit(solution)/shard_map/all_to_all | solution.py:92
  350.7 42.6 %copy-start.12 = (bf16[2048,64]{0,1:T(8,128)(2,1)S(1)}, bf16[2048,64]{0,1:T(8,128)(2,1)}, u32[]{:S(2)}) copy-start(bf16[2048,64]{0,1:T(8,128)(2,1)} %param.13) | copy-start | bytes 786436
  386.8 46.0 %all-to-all-start.4 = ((bf16[64,24,512]{2,1,0:T(8,128)(2,1)}), bf16[64,24,512]{2,1,0:T(8,128)(2,1)}, u32[]{:S(2)}, u32[]{:S(2)}) async-start(bf16[64,24,512]{2,1,0:T(8,128)(2,1)} %bitcast.103), calls=%async_computation.8 | async-start | bytes 3145728 | tf_op jit(solution)/shard_map/all_to_all | solution.py:92
  393.0 73.1 %all-gather.2.cloned.1.call-start = ((), (), s32[]{:S(2)}) async-start(), calls=%async_computation.16 | async-start | bytes 2621440 | tf_op jit(solution)/shard_map/all_gather | solution.py:104
  393.3 1.5 copy-start.4
  393.8 7.5 %copy-start.6 = (f32[128,64]{0,1:T(8,128)}, f32[128,64]{0,1:T(8,128)S(1)}, u32[]{:S(2)}) copy-start(f32[128,64]{0,1:T(8,128)S(1)} %select_reduce_fusion) | copy-start | bytes 98308
  399.4 33.3 %copy-start.5 = (s32[64,128]{1,0:T(8,128)S(1)}, s32[64,128]{1,0:T(8,128)}, u32[]{:S(2)}) copy-start(s32[64,128]{1,0:T(8,128)} %copy-done.3) | copy-start | bytes 98308
  403.1 31.5 %copy-start.7 = (f32[128,64]{0,1:T(8,128)S(1)}, f32[128,64]{0,1:T(8,128)}, u32[]{:S(2)}) copy-start(f32[128,64]{0,1:T(8,128)} %copy-done.6) | copy-start | bytes 98308
  434.6 2.0 copy-start.10
Sparse Core Ops, SparseCore 0:
  10.8 28.6 reduce-scatter.4
  58.3 24.2 reduce-scatter.6
  103.7 24.2 reduce-scatter.8
  149.4 24.2 reduce-scatter.10
  437.7 28.3 all-gather.1

commit v2 on v1

v2 whole, which is shorter than its diff:
```python
import jax
import jax.numpy as jnp
from jax import lax
from jax.sharding import PartitionSpec as P

EPS = 1e-05


def rms_scale(values, gain_vector):
    mean_square = jnp.mean(values * values, axis=-1, keepdims=True)
    return values * lax.rsqrt(mean_square + EPS) * gain_vector


def split_hi_lo(values):
    high = values.astype(jnp.bfloat16)
    low = (values - high.astype(jnp.float32)).astype(jnp.bfloat16)
    return high, low


def local(attn_heads, w_out, residual, moe_gain, router, expert_ids, w_gate_up, w_down, next_gain):
    groups, tok_rows, quarter = attn_heads.shape
    feat_width = w_out.shape[1]
    experts = router.shape[1]
    top_count = expert_ids.shape[1]
    capacity = min(tok_rows, 3 * tok_rows * top_count // (2 * experts))
    slots = experts * capacity

    flat_heads = attn_heads.reshape(groups * tok_rows, quarter)
    partial = jnp.dot(flat_heads, w_out, preferred_element_type=jnp.float32)
    pieces = lax.all_to_all(
        partial.reshape(groups, tok_rows, feat_width), "dp", split_axis=0, concat_axis=0, tiled=True
    )
    projected = jnp.sum(pieces, axis=0)
    mid_wide = (residual.astype(jnp.float32) + projected).astype(jnp.bfloat16).astype(jnp.float32)
    normed = rms_scale(mid_wide, moe_gain).astype(jnp.bfloat16)
    logits = jnp.dot(normed, router, preferred_element_type=jnp.float32)

    expert_pos = jnp.arange(experts, dtype=jnp.int32)
    chosen = expert_ids[:, :, None] == expert_pos[None, None, :]
    member = jnp.sum(chosen.astype(jnp.float32), axis=1)
    row_pos = jnp.arange(tok_rows, dtype=jnp.int32)
    earlier = (row_pos[None, :] < row_pos[:, None]).astype(jnp.bfloat16)
    row_ranks = jnp.dot(
        earlier, member.astype(jnp.bfloat16), preferred_element_type=jnp.float32
    ).astype(jnp.int32)
    slot_pos = jnp.arange(capacity, dtype=jnp.int32)
    placed = (member.T[:, None, :] > 0) & (row_ranks.T[:, None, :] == slot_pos[None, :, None])
    dispatch = placed.reshape(slots, tok_rows).astype(jnp.bfloat16)

    picked = jnp.sum(jnp.where(chosen, logits[:, None, :], 0.0), axis=2)
    raised = jnp.exp(picked)
    gate_weights = raised / jnp.sum(raised, axis=1, keepdims=True)
    weight_full = jnp.sum(jnp.where(chosen, gate_weights[:, :, None], 0.0), axis=1)
    combine = jnp.where(placed, weight_full.T[:, None, :], 0.0).reshape(slots, tok_rows)
    combine_hi, combine_lo = split_hi_lo(combine)

    outgoing = jnp.dot(dispatch, normed, preferred_element_type=jnp.float32).astype(jnp.bfloat16)
    arrived = lax.all_to_all(
        outgoing.reshape(experts, capacity, feat_width), "tp", split_axis=0, concat_axis=0, tiled=True
    ).reshape(slots, feat_width)

    gate_up = w_gate_up[0]
    down_proj = w_down[0]
    hidden_width = down_proj.shape[0]
    projected_up = jnp.dot(arrived, gate_up, preferred_element_type=jnp.float32)
    activated = (
        jax.nn.silu(projected_up[:, :hidden_width]) * projected_up[:, hidden_width:]
    ).astype(jnp.bfloat16)
    served = jnp.dot(activated, down_proj, preferred_element_type=jnp.float32).astype(jnp.bfloat16)

    returned = lax.all_to_all(
        served.reshape(experts, capacity, feat_width), "tp", split_axis=0, concat_axis=0, tiled=True
    ).reshape(slots, feat_width)
    dims = (((0,), (0,)), ((), ()))
    expert_sum = lax.dot_general(
        combine_hi, returned, dims, preferred_element_type=jnp.float32
    ) + lax.dot_general(combine_lo, returned, dims, preferred_element_type=jnp.float32)

    layer_sum = mid_wide + expert_sum
    layer_out = layer_sum.astype(jnp.bfloat16)
    next_local = rms_scale(layer_sum, next_gain).astype(jnp.bfloat16)
    copies = jnp.broadcast_to(next_local[None], (groups, tok_rows, feat_width))
    next_input = lax.all_to_all(copies, "dp", split_axis=0, concat_axis=0, tiled=True)
    return (layer_out, next_input)


def solution(mesh):
    in_specs = (
        P(None, "tp", "dp"),
        P("dp", None),
        P(("dp", "tp"), None),
        P(),
        P(),
        P(("dp", "tp"), None),
        P("tp", None, None),
        P("tp", None, None),
        P(),
    )
    out_specs = (P(("dp", "tp"), None), P(None, "tp", None))
    return jax.shard_map(local, mesh=mesh, in_specs=in_specs, out_specs=out_specs, check_vma=False)
```

time: 477 us -> 412 us (0.86)
  blocking collectives: 45.9 us -> 331 us
  waiting for transfers between devices: 297 us -> 47 us
  starting transfers between devices: 49.9 us -> 5 us
  matrix products: 52.3 us -> 20.4 us
  between operations: 14.2 us -> 0.79 us
  other arithmetic: 12.1 us -> 5.34 us
    all_to_all x1 -> x3, blocking collectives: 45.9 us -> 331 us  [the longest x1 156 us: local(): lax.all_to_all(outgoing.reshape(experts, capacity, feat_width), 'tp', spl...]
    all_to_all x7 -> x1, waiting for transfers between devices: 166 us -> 47 us  [local(): lax.all_to_all(partial.reshape(groups, tok_rows, feat_width), 'dp', split...]
    reduce_scatter x4 -> x0, waiting for transfers between devices: 101 us -> none  [the longest x3 76.3 us: local(): part = lax.psum_scatter(following, 'dp', scatter_dimension=0, tiled=True)]
    all_to_all x7 -> x1, starting transfers between devices: 49.7 us -> 5 us  [local(): lax.all_to_all(partial.reshape(groups, tok_rows, feat_width), 'dp', split...]
    all_gather x1 -> x0, waiting for transfers between devices: 27.7 us -> none  [local(): next_input = lax.all_gather(next_local[None], 'dp', axis=0, tiled=True)]
    dot_general x13 -> x4, matrix products: 39.8 us -> 17.6 us  [the longest x1 6.9 us: local(): projected_up = jnp.dot(arrived, gate_up, preferred_element_type=jnp.float32)]
    convert_element_type x7 -> x0, other arithmetic: 6.78 us -> none  [the longest x4 3.9 us: local(): mid_c = (res_c.astype(jnp.float32) + part).astype(jnp.bfloat16)]
    dot_general x4 -> x1, matrix products: 5.99 us -> 1.12 us  [local(): lax.dot_general(combine_lo, returned, dims, preferred_element_type=jnp.fl...]
  transfers between devices with their start and end apart: 12 -> 1, of which waited for: 12 -> 1; matrix products, arithmetic and copies ran while one was open for 8% -> 0% of each run, Pallas kernels for 0% -> 0%
where the time goes in v2:
time: 412 us; the launch traced here: 411 us
  blocking collectives  331 us (80%)
  waiting for transfers between devices  47 us (11%)
  matrix products  20.4 us (5%)
  other arithmetic  5.34 us (1%)
  starting transfers between devices  5 us (1%)
    all_to_all x1, blocking collectives, local(): lax.all_to_all(outgoing.reshape(experts, capacity, feat_width), 'tp', spl...  156 us
    all_to_all x1, blocking collectives, local(): lax.all_to_all(served.reshape(experts, capacity, feat_width), 'tp', split...  147 us
    all_to_all x1, waiting for transfers between devices, local(): lax.all_to_all(partial.reshape(groups, tok_rows, feat_width), 'dp', split...  47 us
    all_to_all x1, blocking collectives, local(): lax.all_to_all(copies, 'dp', split_axis=0, concat_axis=0, tiled=True)  28.5 us
  transfers between devices with their start and end apart: 1, of which 1 were waited for; matrix products, arithmetic and copies ran while one was open for 0% of the time, Pallas kernels for 0%

profile of v2, /device:TPU:1, one launch (start us, length us, event | category | flops | bytes accessed | tf_op | source)
XLA Modules:
  0.0 411.5 jit_solution(12170305370913618576)
XLA Ops:
  0.6 0.0 copy-start
  0.6 5.1 %fusion.6 = f32[4,128,2048]{2,1,0:T(8,128)} fusion(bf16[4,128,512]{2,1,0:T(8,128)(2,1)} %param.9, bf16[512,2048]{1,0:T(8,128)(2,1)} %param.10), kind=kOutput, calls=%fused_computation.11 | convolution fusion | flops 1073741824 | bytes 6815744 | tf_op jit(solution)/shard_map/dot_general | solution.py:29
  5.8 5.0 %all-to-all-start = ((f32[4,128,2048]{2,1,0:T(8,128)}), f32[4,128,2048]{2,1,0:T(8,128)}, u32[]{:S(2)}, u32[]{:S(2)}) async-start(f32[4,128,2048]{2,1,0:T(8,128)} %fusion.6), calls=%async_computation | async-start | bytes 8388608 | tf_op jit(solution)/shard_map/all_to_all | solution.py:30
  10.8 0.0 copy-start.2
  10.8 0.0 copy-start.5
  10.8 0.1 eq.48
  10.9 0.0 copy-start.1
  10.9 47.0 %all-to-all-done = f32[4,128,2048]{2,1,0:T(8,128)} async-done(((f32[4,128,2048]{2,1,0:T(8,128)}), f32[4,128,2048]{2,1,0:T(8,128)}, u32[]{:S(2)}, u32[]{:S(2)}) %all-to-all-start) | async-done | bytes 4194336 | tf_op jit(solution)/shard_map/all_to_all | solution.py:30
  57.9 2.6 reduce_sum.63
  60.5 1.3 fusion.10
  61.8 0.0 copy-done.2
  61.8 0.0 copy-done.5
  61.8 0.4 fusion.26
  62.2 0.0 copy-done.1
  62.3 0.1 select_reduce_fusion
  62.4 0.1 convolution_convert_fusion.2
  62.5 0.3 fusion.15
  62.8 1.9 convolution_convert_fusion.1
  64.7 0.0 copy-start.4
  64.7 156.0 %all_to_all.20 = bf16[64,24,2048]{2,1,0:T(8,128)(2,1)S(1)} all-to-all(bf16[64,24,2048]{2,1,0:T(8,128)(2,1)S(1)} %bitcast.35), channel_id=1, replica_groups=mesh['dp'=4,'tp'=64] {'tp'}, dimensions={0} | all-to-all | bytes 12582912 | tf_op jit(solution)/shard_map/all_to_all | solution.py:58
  220.7 0.0 copy-done.4
  220.7 6.9 %fusion = f32[1536,1024]{1,0:T(8,128)S(1)} fusion(bf16[1536,2048]{1,0:T(8,128)(2,1)S(1)} %bitcast.36, bf16[1,2048,1024]{2,1,0:T(8,128)(2,1)S(1)} %copy-done.4), kind=kOutput, calls=%fused_computation.2 | convolution fusion | flops 6442450944 | bytes 16777216 | tf_op jit(solution)/shard_map/dot_general | solution.py:65
  227.6 0.0 copy-done
  227.6 3.7 convolution_convert_fusion
  231.3 146.7 %all_to_all.21 = bf16[64,24,2048]{2,1,0:T(8,128)(2,1)S(1)} all-to-all(bf16[64,24,2048]{2,1,0:T(8,128)(2,1)S(1)} %bitcast.37), channel_id=1, replica_groups=mesh['dp'=4,'tp'=64] {'tp'}, dimensions={0} | all-to-all | bytes 12582912 | tf_op jit(solution)/shard_map/all_to_all | solution.py:71
  378.0 1.1 convolution_bitcast_fusion
  379.1 0.0 copy-start.3
  379.1 1.2 multiply_reduce_fusion
  380.3 0.0 copy-done.3
  380.3 1.0 multiply_convert_fusion
  381.4 0.3 broadcast_in_dim.41
  381.6 28.5 %all_to_all.22 = bf16[4,128,2048]{2,1,0:T(8,128)(2,1)S(1)} all-to-all(bf16[4,128,2048]{2,1,0:T(8,128)(2,1)S(1)} %broadcast_in_dim.41), channel_id=1, replica_groups=mesh['dp'=4,'tp'=64] {'dp'}, dimensions={0} | all-to-all | bytes 4194304 | tf_op jit(solution)/shard_map/all_to_all | solution.py:83
  410.1 1.3 copy.24
  (7 shorter events, 0.1 us)
Async XLA Ops:
  0.6 227.0 %copy-start = (bf16[1,512,2048]{2,1,0:T(8,128)(2,1)S(1)}, bf16[1,512,2048]{2,1,0:T(8,128)(2,1)}, u32[]{:S(2)}) copy-start(bf16[1,512,2048]{2,1,0:T(8,128)(2,1)} %param.16) | copy-start | bytes 6291460
  5.8 52.1 %all-to-all-start = ((f32[4,128,2048]{2,1,0:T(8,128)}), f32[4,128,2048]{2,1,0:T(8,128)}, u32[]{:S(2)}, u32[]{:S(2)}) async-start(f32[4,128,2048]{2,1,0:T(8,128)} %fusion.6), calls=%async_computation | async-start | bytes 8388608 | tf_op jit(solution)/shard_map/all_to_all | solution.py:30
  10.8 51.0 %copy-start.2 = (f32[2048]{0:T(1024)S(1)}, f32[2048]{0:T(1024)}, u32[]{:S(2)}) copy-start(f32[2048]{0:T(1024)} %param.12) | copy-start | bytes 24580
  10.8 51.0 %copy-start.5 = (bf16[2048,64]{0,1:T(8,128)(2,1)S(1)}, bf16[2048,64]{0,1:T(8,128)(2,1)}, u32[]{:S(2)}) copy-start(bf16[2048,64]{0,1:T(8,128)(2,1)} %param.13) | copy-start | bytes 786436
  10.9 51.3 %copy-start.1 = (s32[128,8]{0,1:T(8,128)S(1)}, s32[128,8]{0,1:T(8,128)}, u32[]{:S(2)}) copy-start(s32[128,8]{0,1:T(8,128)} %param.14) | copy-start | bytes 12292
  64.7 156.0 %copy-start.4 = (bf16[1,2048,1024]{2,1,0:T(8,128)(2,1)S(1)}, bf16[1,2048,1024]{2,1,0:T(8,128)(2,1)}, u32[]{:S(2)}) copy-start(bf16[1,2048,1024]{2,1,0:T(8,128)(2,1)} %param.15) | copy-start | bytes 12582916
  379.1 1.2 copy-start.3

commit v3 on v2

--- a/solution.py
+++ b/solution.py
@@ -25,16 +25,6 @@
     capacity = min(tok_rows, 3 * tok_rows * top_count // (2 * experts))
     slots = experts * capacity
 
-    flat_heads = attn_heads.reshape(groups * tok_rows, quarter)
-    partial = jnp.dot(flat_heads, w_out, preferred_element_type=jnp.float32)
-    pieces = lax.all_to_all(
-        partial.reshape(groups, tok_rows, feat_width), "dp", split_axis=0, concat_axis=0, tiled=True
-    )
-    projected = jnp.sum(pieces, axis=0)
-    mid_wide = (residual.astype(jnp.float32) + projected).astype(jnp.bfloat16).astype(jnp.float32)
-    normed = rms_scale(mid_wide, moe_gain).astype(jnp.bfloat16)
-    logits = jnp.dot(normed, router, preferred_element_type=jnp.float32)
-
     expert_pos = jnp.arange(experts, dtype=jnp.int32)
     chosen = expert_ids[:, :, None] == expert_pos[None, None, :]
     member = jnp.sum(chosen.astype(jnp.float32), axis=1)
@@ -47,6 +37,36 @@
     placed = (member.T[:, None, :] > 0) & (row_ranks.T[:, None, :] == slot_pos[None, :, None])
     dispatch = placed.reshape(slots, tok_rows).astype(jnp.bfloat16)
 
+    half = feat_width // 2
+    flat_heads = attn_heads.reshape(groups * tok_rows, quarter)
+    partials = [
+        jnp.dot(flat_heads, w_out[:, c * half : (c + 1) * half], preferred_element_type=jnp.float32)
+        for c in range(2)
+    ]
+    pieces = lax.all_to_all(
+        partials[0].reshape(groups, tok_rows, half), "dp", split_axis=0, concat_axis=0, tiled=True
+    )
+    part = jnp.sum(pieces, axis=0)
+    mid_parts = []
+    arrived_parts = []
+    for c in range(2):
+        cols = slice(c * half, (c + 1) * half)
+        res_c, part = lax.optimization_barrier((residual[:, cols], part))
+        mid_c = (res_c.astype(jnp.float32) + part).astype(jnp.bfloat16)
+        mid_parts.append(mid_c)
+        outgoing = jnp.dot(dispatch, mid_c, preferred_element_type=jnp.float32).astype(jnp.bfloat16)
+        if c == 0:
+            outgoing, following = lax.optimization_barrier((outgoing, partials[1]))
+            part = lax.psum_scatter(following, "dp", scatter_dimension=0, tiled=True)
+        arrived_parts.append(
+            lax.all_to_all(
+                outgoing.reshape(experts, capacity, half), "tp", split_axis=0, concat_axis=0, tiled=True
+            ).reshape(slots, half)
+        )
+    mid_wide = jnp.concatenate(mid_parts, axis=1).astype(jnp.float32)
+    normed = rms_scale(mid_wide, moe_gain).astype(jnp.bfloat16)
+    logits = jnp.dot(normed, router, preferred_element_type=jnp.float32)
+
     picked = jnp.sum(jnp.where(chosen, logits[:, None, :], 0.0), axis=2)
     raised = jnp.exp(picked)
     gate_weights = raised / jnp.sum(raised, axis=1, keepdims=True)
@@ -54,10 +74,8 @@
     combine = jnp.where(placed, weight_full.T[:, None, :], 0.0).reshape(slots, tok_rows)
     combine_hi, combine_lo = split_hi_lo(combine)
 
-    outgoing = jnp.dot(dispatch, normed, preferred_element_type=jnp.float32).astype(jnp.bfloat16)
-    arrived = lax.all_to_all(
-        outgoing.reshape(experts, capacity, feat_width), "tp", split_axis=0, concat_axis=0, tiled=True
-    ).reshape(slots, feat_width)
+    arrived_mid = jnp.concatenate(arrived_parts, axis=1).astype(jnp.float32)
+    arrived = rms_scale(arrived_mid, moe_gain).astype(jnp.bfloat16)
 
     gate_up = w_gate_up[0]
     down_proj = w_down[0]

time: 412 us -> 425 us (1.032)
  blocking collectives: 331 us -> 108 us
  waiting for transfers between devices: 47 us -> 228 us
  starting transfers between devices: 5 us -> 26.6 us
  matrix products: 20.4 us -> 34.5 us
  between operations: 0.79 us -> 14.2 us
    all_to_all x2 -> x1, blocking collectives: 303 us -> 79.2 us  [local(): lax.all_to_all(outgoing.reshape(experts, capacity, half), 'tp', split_axi...]
    all_to_all x1 -> x3, waiting for transfers between devices: 47 us -> 193 us  [the longest x1 140 us: local(): lax.all_to_all(served.reshape(experts, capacity, feat_width), 'tp', split...]
    reduce_scatter x0 -> x1, waiting for transfers between devices: none -> 34.6 us  [local(): part = lax.psum_scatter(following, 'dp', scatter_dimension=0, tiled=True)]
    all_to_all x1 -> x3, starting transfers between devices: 5 us -> 26.6 us  [the longest x1 14.9 us: local(): lax.all_to_all(outgoing.reshape(experts, capacity, half), 'tp', split_axi...]
    dot_general x2 -> x4, matrix products: 6.99 us -> 12.1 us  [the longest x2 6.8 us: local(): jnp.dot(flat_heads, w_out[:, c * half:(c + 1) * half], preferred_element_...]
  transfers between devices with their start and end apart: 1 -> 4, of which waited for: 1 -> 4; matrix products, arithmetic and copies ran while one was open for 0% -> 2% of each run, Pallas kernels for 0% -> 0%
where the time goes in v3:
time: 425 us
  waiting for transfers between devices  228 us (54%)
  blocking collectives  108 us (25%)
  matrix products  34.5 us (8%)
  starting transfers between devices  26.6 us (6%)
  between operations  14.2 us (3%)
  other arithmetic  9.19 us (2%)
    all_to_all x1, waiting for transfers between devices, local(): lax.all_to_all(served.reshape(experts, capacity, feat_width), 'tp', split...  140 us
    all_to_all x1, blocking collectives, local(): lax.all_to_all(outgoing.reshape(experts, capacity, half), 'tp', split_axi...  79.2 us
    reduce_scatter x1, waiting for transfers between devices, local(): part = lax.psum_scatter(following, 'dp', scatter_dimension=0, tiled=True)  34.6 us
    all_to_all x1, waiting for transfers between devices, local(): lax.all_to_all(outgoing.reshape(experts, capacity, half), 'tp', split_axi...  34.3 us
    all_to_all x1, blocking collectives, local(): lax.all_to_all(copies, 'dp', split_axis=0, concat_axis=0, tiled=True)  29 us
    all_to_all x1, waiting for transfers between devices, local(): lax.all_to_all(partials[0].reshape(groups, tok_rows, half), 'dp', split_a...  18.7 us
    all_to_all x1, starting transfers between devices, local(): lax.all_to_all(outgoing.reshape(experts, capacity, half), 'tp', split_axi...  14.9 us
    dot_general x1, matrix products, local(): projected_up = jnp.dot(arrived, gate_up, preferred_element_type=jnp.float32)  8.73 us
  transfers between devices with their start and end apart: 4, of which 4 were waited for; matrix products, arithmetic and copies ran while one was open for 2% of the time, Pallas kernels for 0%

profile of v3, /device:TPU:1, one launch (start us, length us, event | category | flops | bytes accessed | tf_op | source)
XLA Modules:
  0.0 424.6 jit_solution(17029557966717258086)
XLA Ops:
  7.2 0.0 copy-start
  7.2 0.0 copy-start.2
  7.2 3.5 fusion.17
  10.7 0.0 copy-start.1
  10.7 5.1 %all-to-all-start = ((f32[4,128,1024]{2,1,0:T(8,128)}), f32[4,128,1024]{2,1,0:T(8,128)}, u32[]{:S(2)}, u32[]{:S(2)}) async-start(f32[4,128,1024]{2,1,0:T(8,128)} %fusion.17), calls=%async_computation | async-start | bytes 4194304 | tf_op jit(solution)/shard_map/all_to_all | solution.py:46
  15.9 0.1 eq.46
  16.0 0.0 copy-done.2
  16.0 0.1 convolution_convert_fusion.3
  16.2 0.3 fusion.24
  16.5 1.8 fusion.44
  18.2 0.0 copy-done.1
  18.2 3.3 fusion.19
  21.5 18.7 %all-to-all-done = f32[4,128,1024]{2,1,0:T(8,128)} async-done(((f32[4,128,1024]{2,1,0:T(8,128)}), f32[4,128,1024]{2,1,0:T(8,128)}, u32[]{:S(2)}, u32[]{:S(2)}) %all-to-all-start) | async-done | bytes 2097184 | tf_op jit(solution)/shard_map/all_to_all | solution.py:46
  40.2 1.8 reduce_sum.72
  42.0 1.0 add_convert_fusion.1
  43.0 2.7 convolution_convert_fusion.2
  45.7 14.9 %all-to-all-start.1 = ((bf16[64,24,1024]{2,1,0:T(8,128)(2,1)}), bf16[64,24,1024]{2,1,0:T(8,128)(2,1)}, u32[]{:S(2)}, u32[]{:S(2)}) async-start(bf16[64,24,1024]{2,1,0:T(8,128)(2,1)} %bitcast.41), calls=%async_computation.2 | async-start | bytes 6291456 | tf_op jit(solution)/shard_map/all_to_all | solution.py:62
  60.6 0.0 reduce-scatter.2.cloned.1.call-start
  60.7 0.7 reduce-scatter.2.cloned.1.call-update
  61.4 34.6 %reduce-scatter.2.cloned.1.call-done = f32[128,1024]{1,0:T(8,128)} async-done(((f32[512,1024]{1,0:T(8,128)}), f32[128,1024]{1,0:T(8,128)}) %reduce-scatter.2.cloned.1.call-update) | async-done | bytes 524304 | tf_op jit(solution)/shard_map/reduce_scatter | solution.py:60
  95.9 1.1 add_convert_fusion
  97.0 2.7 convolution_convert_fusion.1
  99.7 34.3 %all-to-all-done.1 = bf16[64,24,1024]{2,1,0:T(8,128)(2,1)} async-done(((bf16[64,24,1024]{2,1,0:T(8,128)(2,1)}), bf16[64,24,1024]{2,1,0:T(8,128)(2,1)}, u32[]{:S(2)}, u32[]{:S(2)}) %all-to-all-start.1) | async-done | bytes 3145760 | tf_op jit(solution)/shard_map/all_to_all | solution.py:62
  134.0 79.2 %all_to_all.25 = bf16[64,24,1024]{2,1,0:T(8,128)(2,1)S(1)} all-to-all(bf16[64,24,1024]{2,1,0:T(8,128)(2,1)} %bitcast.42), channel_id=1, replica_groups=mesh['dp'=4,'tp'=64] {'tp'}, dimensions={0} | all-to-all | bytes 6291456 | tf_op jit(solution)/shard_map/all_to_all | solution.py:62
  213.2 0.0 copy-start.4
  213.2 0.0 copy-start.6
  213.2 3.6 fusion
  216.9 0.0 copy-done.4
  216.9 0.0 copy-done.6
  216.9 8.7 %fusion.3 = f32[1536,1024]{1,0:T(8,128)S(1)} fusion(f32[2048]{0:T(1024)S(1)} %copy-done.6, f32[1536]{0:T(1024)S(1)} %add_rsqrt_fusion, bf16[1,2048,1024]{2,1,0:T(8,128)(2,1)S(1)} %copy-done.4, bf16[1536,1024]{1,0:T(8,128)(2,1)S(1)} %bitcast.44, bf16[1536,1024]{1,0:T(8,128)(2,1)} %bitcast.7), kind=kOutput, calls=%fused_computation.6 | convolution fusion | flops 6464471040 | bytes 16791552 | tf_op jit(solution)/shard_map/dot_general | solution.py:83
  225.6 0.0 copy-done
  225.6 5.3 %convolution_convert_fusion = bf16[1536,2048]{1,0:T(8,128)(2,1)} fusion(bf16[1,512,2048]{2,1,0:T(8,128)(2,1)S(1)} %copy-done, f32[1536,1024]{1,0:T(8,128)S(1)} %fusion.3), kind=kOutput, calls=%fused_computation.5 | convolution fusion | flops 3229089792 | bytes 14680064 | tf_op jit(solution)/shard_map/dot_general | solution.py:87
  231.0 0.0 copy-start.5
  231.0 6.5 %all-to-all-start.3 = ((bf16[64,24,2048]{2,1,0:T(8,128)(2,1)}), bf16[64,24,2048]{2,1,0:T(8,128)(2,1)}, u32[]{:S(2)}, u32[]{:S(2)}) async-start(bf16[64,24,2048]{2,1,0:T(8,128)(2,1)} %bitcast.45), calls=%async_computation.4 | async-start | bytes 12582912 | tf_op jit(solution)/shard_map/all_to_all | solution.py:89
  237.5 0.2 fusion.14
  237.7 0.0 copy-done.5
  237.7 0.4 fusion.25
  238.2 140.1 %all-to-all-done.3 = bf16[64,24,2048]{2,1,0:T(8,128)(2,1)} async-done(((bf16[64,24,2048]{2,1,0:T(8,128)(2,1)}), bf16[64,24,2048]{2,1,0:T(8,128)(2,1)}, u32[]{:S(2)}, u32[]{:S(2)}) %all-to-all-start.3) | async-done | bytes 6291488 | tf_op jit(solution)/shard_map/all_to_all | solution.py:89
  378.3 3.8 convolution_bitcast_fusion
  382.1 0.0 copy-start.3
  382.1 3.9 multiply_reduce_fusion
  386.1 0.0 copy-done.3
  386.1 1.0 multiply_convert_fusion
  387.1 0.2 broadcast_in_dim.41
  387.4 29.0 %all_to_all.26 = bf16[4,128,2048]{2,1,0:T(8,128)(2,1)S(1)} all-to-all(bf16[4,128,2048]{2,1,0:T(8,128)(2,1)S(1)} %broadcast_in_dim.41), channel_id=1, replica_groups=mesh['dp'=4,'tp'=64] {'dp'}, dimensions={0} | all-to-all | bytes 4194304 | tf_op jit(solution)/shard_map/all_to_all | solution.py:101
  416.4 1.3 copy.25
  (10 shorter events, 0.2 us)
Async XLA Ops:
  7.2 218.5 %copy-start = (bf16[1,512,2048]{2,1,0:T(8,128)(2,1)S(1)}, bf16[1,512,2048]{2,1,0:T(8,128)(2,1)}, u32[]{:S(2)}) copy-start(bf16[1,512,2048]{2,1,0:T(8,128)(2,1)} %param.16) | copy-start | bytes 6291460
  7.2 8.8 %copy-start.2 = (s32[128,8]{0,1:T(8,128)S(1)}, s32[128,8]{0,1:T(8,128)}, u32[]{:S(2)}) copy-start(s32[128,8]{0,1:T(8,128)} %param.14) | copy-start | bytes 12292
  10.7 7.5 %copy-start.1 = (bf16[4,128,512]{2,1,0:T(8,128)(2,1)S(1)}, bf16[4,128,512]{2,1,0:T(8,128)(2,1)}, u32[]{:S(2)}) copy-start(bf16[4,128,512]{2,1,0:T(8,128)(2,1)} %param.9) | copy-start | bytes 1572868
  10.7 29.5 %all-to-all-start = ((f32[4,128,1024]{2,1,0:T(8,128)}), f32[4,128,1024]{2,1,0:T(8,128)}, u32[]{:S(2)}, u32[]{:S(2)}) async-start(f32[4,128,1024]{2,1,0:T(8,128)} %fusion.17), calls=%async_computation | async-start | bytes 4194304 | tf_op jit(solution)/shard_map/all_to_all | solution.py:46
  45.7 88.3 %all-to-all-start.1 = ((bf16[64,24,1024]{2,1,0:T(8,128)(2,1)}), bf16[64,24,1024]{2,1,0:T(8,128)(2,1)}, u32[]{:S(2)}, u32[]{:S(2)}) async-start(bf16[64,24,1024]{2,1,0:T(8,128)(2,1)} %bitcast.41), calls=%async_computation.2 | async-start | bytes 6291456 | tf_op jit(solution)/shard_map/all_to_all | solution.py:62
  60.6 35.3 %reduce-scatter.2.cloned.1.call-start = ((), (), s32[]{:S(2)}) async-start(), calls=%async_computation.6 | async-start | bytes 2621440 | tf_op jit(solution)/shard_map/reduce_scatter | solution.py:60
  213.2 3.6 copy-start.4
  213.2 3.6 copy-start.6
  231.0 6.7 %copy-start.5 = (bf16[2048,64]{0,1:T(8,128)(2,1)S(1)}, bf16[2048,64]{0,1:T(8,128)(2,1)}, u32[]{:S(2)}) copy-start(bf16[2048,64]{0,1:T(8,128)(2,1)} %param.13) | copy-start | bytes 786436
  231.0 147.3 %all-to-all-start.3 = ((bf16[64,24,2048]{2,1,0:T(8,128)(2,1)}), bf16[64,24,2048]{2,1,0:T(8,128)(2,1)}, u32[]{:S(2)}, u32[]{:S(2)}) async-start(bf16[64,24,2048]{2,1,0:T(8,128)(2,1)} %bitcast.45), calls=%async_computation.4 | async-start | bytes 12582912 | tf_op jit(solution)/shard_map/all_to_all | solution.py:89
  382.1 4.0 copy-start.3
Sparse Core Ops, SparseCore 0:
  64.6 31.3 reduce-scatter.1

commit v4 on v3

--- a/solution.py
+++ b/solution.py
@@ -15,6 +15,17 @@
     high = values.astype(jnp.bfloat16)
     low = (values - high.astype(jnp.float32)).astype(jnp.bfloat16)
     return high, low
+
+
+def dp_reduce(blocks):
+    ring = blocks.shape[0]
+    here = lax.axis_index("dp")
+    total = blocks[here]
+    for shift in range(1, ring):
+        sent = lax.dynamic_index_in_dim(blocks, (here + shift) % ring, axis=0, keepdims=False)
+        pairs = [(j, (j + shift) % ring) for j in range(ring)]
+        total = total + lax.ppermute(sent, "dp", pairs)
+    return total
 
 
 def local(attn_heads, w_out, residual, moe_gain, router, expert_ids, w_gate_up, w_down, next_gain):
@@ -57,7 +68,7 @@
         outgoing = jnp.dot(dispatch, mid_c, preferred_element_type=jnp.float32).astype(jnp.bfloat16)
         if c == 0:
             outgoing, following = lax.optimization_barrier((outgoing, partials[1]))
-            part = lax.psum_scatter(following, "dp", scatter_dimension=0, tiled=True)
+            part = dp_reduce(following.reshape(groups, tok_rows, half))
         arrived_parts.append(
             lax.all_to_all(
                 outgoing.reshape(experts, capacity, half), "tp", split_axis=0, concat_axis=0, tiled=True

time: 425 us -> 412 us (0.969)
  between operations: 14.2 us -> 0.88 us
  waiting for transfers between devices: 228 us -> 223 us
    reduce_scatter x1 -> x0, waiting for transfers between devices: 34.6 us -> none  [local(): part = lax.psum_scatter(following, 'dp', scatter_dimension=0, tiled=True)]
    ppermute x0 -> x3, waiting for transfers between devices: none -> 25.6 us  [dp_reduce(): total = total + lax.ppermute(sent, 'dp', pairs)]
    all_to_all x1, waiting for transfers between devices: 34.3 us -> 38.7 us  [local(): lax.all_to_all(outgoing.reshape(experts, capacity, half), 'tp', split_axi...]
  transfers between devices with their start and end apart: 4 -> 6, of which waited for: 4 -> 6; matrix products, arithmetic and copies ran while one was open for 2% -> 3% of each run, Pallas kernels for 0% -> 0%
where the time goes in v4:
time: 412 us; the launch traced here: 411 us
  waiting for transfers between devices  223 us (54%)
  blocking collectives  108 us (26%)
  matrix products  34.5 us (8%)
  starting transfers between devices  28.7 us (7%)
  other arithmetic  9.81 us (2%)
  local copies, waits for them, and re-layouts  5.97 us (1%)
    all_to_all x1, waiting for transfers between devices, local(): lax.all_to_all(served.reshape(experts, capacity, feat_width), 'tp', split...  140 us
    all_to_all x1, blocking collectives, local(): lax.all_to_all(outgoing.reshape(experts, capacity, half), 'tp', split_axi...  79.2 us
    all_to_all x1, waiting for transfers between devices, local(): lax.all_to_all(outgoing.reshape(experts, capacity, half), 'tp', split_axi...  38.7 us
    all_to_all x1, blocking collectives, local(): lax.all_to_all(copies, 'dp', split_axis=0, concat_axis=0, tiled=True)  29 us
    ppermute x3, waiting for transfers between devices, dp_reduce(): total = total + lax.ppermute(sent, 'dp', pairs)  25.6 us
    all_to_all x1, waiting for transfers between devices, local(): lax.all_to_all(partials[0].reshape(groups, tok_rows, half), 'dp', split_a...  18.7 us
    all_to_all x1, starting transfers between devices, local(): lax.all_to_all(outgoing.reshape(experts, capacity, half), 'tp', split_axi...  14.9 us
    dot_general x1, matrix products, local(): projected_up = jnp.dot(arrived, gate_up, preferred_element_type=jnp.float32)  8.73 us
  transfers between devices with their start and end apart: 6, of which 6 were waited for; matrix products, arithmetic and copies ran while one was open for 3% of the time, Pallas kernels for 0%

profile of v4, /device:TPU:1, one launch (start us, length us, event | category | flops | bytes accessed | tf_op | source)
XLA Modules:
  0.0 411.2 jit_solution(16516205500196170478)
XLA Ops:
  0.6 0.0 copy-start
  0.6 0.0 copy-start.2
  0.7 3.5 fusion.17
  4.2 0.0 copy-start.1
  4.2 5.1 %all-to-all-start = ((f32[4,128,1024]{2,1,0:T(8,128)}), f32[4,128,1024]{2,1,0:T(8,128)}, u32[]{:S(2)}, u32[]{:S(2)}) async-start(f32[4,128,1024]{2,1,0:T(8,128)} %fusion.17), calls=%async_computation | async-start | bytes 4194304 | tf_op jit(solution)/shard_map/all_to_all | solution.py:57
  9.3 0.1 eq.50
  9.4 0.0 copy-done.2
  9.5 0.1 convolution_convert_fusion.3
  9.6 0.3 fusion.24
  9.9 1.8 fusion.46
  11.7 0.0 copy-done.1
  11.7 3.3 fusion.19
  15.0 18.7 %all-to-all-done = f32[4,128,1024]{2,1,0:T(8,128)} async-done(((f32[4,128,1024]{2,1,0:T(8,128)}), f32[4,128,1024]{2,1,0:T(8,128)}, u32[]{:S(2)}, u32[]{:S(2)}) %all-to-all-start) | async-done | bytes 2097184 | tf_op jit(solution)/shard_map/all_to_all | solution.py:57
  33.7 1.8 reduce_sum.72
  35.5 1.0 add_convert_fusion.1
  36.5 2.7 convolution_convert_fusion.2
  39.2 14.9 %all-to-all-start.1 = ((bf16[64,24,1024]{2,1,0:T(8,128)(2,1)}), bf16[64,24,1024]{2,1,0:T(8,128)(2,1)}, u32[]{:S(2)}, u32[]{:S(2)}) async-start(bf16[64,24,1024]{2,1,0:T(8,128)(2,1)} %bitcast.54), calls=%async_computation.1 | async-start | bytes 6291456 | tf_op jit(solution)/shard_map/all_to_all | solution.py:73
  54.1 2.5 dynamic-slice_bitcast_fusion.2
  56.6 0.9 collective-permute-start.2
  57.5 1.3 collective-permute-start.1
  58.8 0.0 collective-permute-start
  58.8 11.1 %collective-permute-done.2 = f32[128,1024]{1,0:T(8,128)} collective-permute-done((f32[128,1024]{1,0:T(8,128)}, f32[128,1024]{1,0:T(8,128)}, u32[]{:S(2)}, u32[]{:S(2)}) %collective-permute-start.2) | collective-permute-done | bytes 524320 | tf_op jit(solution)/shard_map/ppermute | solution.py:27
  69.9 2.2 collective-permute-done.1
  72.1 12.4 %collective-permute-done = f32[128,1024]{1,0:T(8,128)} collective-permute-done((f32[128,1024]{1,0:T(8,128)S(1)}, f32[128,1024]{1,0:T(8,128)}, u32[]{:S(2)}, u32[]{:S(2)}) %collective-permute-start) | collective-permute-done | bytes 524320 | tf_op jit(solution)/shard_map/ppermute | solution.py:27
  84.4 1.7 fusion.28
  86.1 0.1 add_convert_fusion
  86.1 2.7 convolution_convert_fusion.1
  88.8 38.7 %all-to-all-done.1 = bf16[64,24,1024]{2,1,0:T(8,128)(2,1)} async-done(((bf16[64,24,1024]{2,1,0:T(8,128)(2,1)}), bf16[64,24,1024]{2,1,0:T(8,128)(2,1)}, u32[]{:S(2)}, u32[]{:S(2)}) %all-to-all-start.1) | async-done | bytes 3145760 | tf_op jit(solution)/shard_map/all_to_all | solution.py:73
  127.5 79.2 %all_to_all.25 = bf16[64,24,1024]{2,1,0:T(8,128)(2,1)S(1)} all-to-all(bf16[64,24,1024]{2,1,0:T(8,128)(2,1)} %bitcast.55), channel_id=1, replica_groups=mesh['dp'=4,'tp'=64] {'tp'}, dimensions={0} | all-to-all | bytes 6291456 | tf_op jit(solution)/shard_map/all_to_all | solution.py:73
  206.7 3.6 fusion
  210.3 0.0 copy-done.4
  210.3 0.0 copy-done.6
  210.4 8.7 %fusion.3 = f32[1536,1024]{1,0:T(8,128)S(1)} fusion(f32[2048]{0:T(1024)S(1)} %copy-done.6, f32[1536]{0:T(1024)S(1)} %add_rsqrt_fusion, bf16[1,2048,1024]{2,1,0:T(8,128)(2,1)S(1)} %copy-done.4, bf16[1536,1024]{1,0:T(8,128)(2,1)S(1)} %bitcast.57, bf16[1536,1024]{1,0:T(8,128)(2,1)} %bitcast.12), kind=kOutput, calls=%fused_computation.6 | convolution fusion | flops 6464471040 | bytes 16791552 | tf_op jit(solution)/shard_map/dot_general | solution.py:94
  219.1 0.0 copy-done
  219.1 5.3 %convolution_convert_fusion = bf16[1536,2048]{1,0:T(8,128)(2,1)} fusion(bf16[1,512,2048]{2,1,0:T(8,128)(2,1)S(1)} %copy-done, f32[1536,1024]{1,0:T(8,128)S(1)} %fusion.3), kind=kOutput, calls=%fused_computation.5 | convolution fusion | flops 3229089792 | bytes 14680064 | tf_op jit(solution)/shard_map/dot_general | solution.py:98
  224.4 6.5 %all-to-all-start.3 = ((bf16[64,24,2048]{2,1,0:T(8,128)(2,1)}), bf16[64,24,2048]{2,1,0:T(8,128)(2,1)}, u32[]{:S(2)}, u32[]{:S(2)}) async-start(bf16[64,24,2048]{2,1,0:T(8,128)(2,1)} %bitcast.60), calls=%async_computation.3 | async-start | bytes 12582912 | tf_op jit(solution)/shard_map/all_to_all | solution.py:100
  230.9 0.2 fusion.14
  231.1 0.0 copy-done.5
  231.1 0.4 fusion.25
  231.6 140.1 %all-to-all-done.3 = bf16[64,24,2048]{2,1,0:T(8,128)(2,1)} async-done(((bf16[64,24,2048]{2,1,0:T(8,128)(2,1)}), bf16[64,24,2048]{2,1,0:T(8,128)(2,1)}, u32[]{:S(2)}, u32[]{:S(2)}) %all-to-all-start.3) | async-done | bytes 6291488 | tf_op jit(solution)/shard_map/all_to_all | solution.py:100
  371.7 3.8 convolution_bitcast_fusion
  375.6 0.0 copy-start.3
  375.6 3.9 multiply_reduce_fusion
  379.6 0.0 copy-done.3
  379.6 1.0 multiply_convert_fusion
  380.6 0.3 broadcast_in_dim.41
  380.9 29.0 %all_to_all.26 = bf16[4,128,2048]{2,1,0:T(8,128)(2,1)S(1)} all-to-all(bf16[4,128,2048]{2,1,0:T(8,128)(2,1)S(1)} %broadcast_in_dim.41), channel_id=1, replica_groups=mesh['dp'=4,'tp'=64] {'dp'}, dimensions={0} | all-to-all | bytes 4194304 | tf_op jit(solution)/shard_map/all_to_all | solution.py:112
  409.9 1.3 copy.25
  (13 shorter events, 0.2 us)
Async XLA Ops:
  0.6 218.5 %copy-start = (bf16[1,512,2048]{2,1,0:T(8,128)(2,1)S(1)}, bf16[1,512,2048]{2,1,0:T(8,128)(2,1)}, u32[]{:S(2)}) copy-start(bf16[1,512,2048]{2,1,0:T(8,128)(2,1)} %param.16) | copy-start | bytes 6291460
  0.6 8.8 %copy-start.2 = (s32[128,8]{0,1:T(8,128)S(1)}, s32[128,8]{0,1:T(8,128)}, u32[]{:S(2)}) copy-start(s32[128,8]{0,1:T(8,128)} %param.14) | copy-start | bytes 12292
  4.2 7.5 %copy-start.1 = (bf16[4,128,512]{2,1,0:T(8,128)(2,1)S(1)}, bf16[4,128,512]{2,1,0:T(8,128)(2,1)}, u32[]{:S(2)}) copy-start(bf16[4,128,512]{2,1,0:T(8,128)(2,1)} %param.9) | copy-start | bytes 1572868
  4.2 29.5 %all-to-all-start = ((f32[4,128,1024]{2,1,0:T(8,128)}), f32[4,128,1024]{2,1,0:T(8,128)}, u32[]{:S(2)}, u32[]{:S(2)}) async-start(f32[4,128,1024]{2,1,0:T(8,128)} %fusion.17), calls=%async_computation | async-start | bytes 4194304 | tf_op jit(solution)/shard_map/all_to_all | solution.py:57
  39.2 88.3 %all-to-all-start.1 = ((bf16[64,24,1024]{2,1,0:T(8,128)(2,1)}), bf16[64,24,1024]{2,1,0:T(8,128)(2,1)}, u32[]{:S(2)}, u32[]{:S(2)}) async-start(bf16[64,24,1024]{2,1,0:T(8,128)(2,1)} %bitcast.54), calls=%async_computation.1 | async-start | bytes 6291456 | tf_op jit(solution)/shard_map/all_to_all | solution.py:73
  56.6 13.3 %collective-permute-start.2 = (f32[128,1024]{1,0:T(8,128)}, f32[128,1024]{1,0:T(8,128)}, u32[]{:S(2)}, u32[]{:S(2)}) collective-permute-start(f32[128,1024]{1,0:T(8,128)} %get-tuple-element.15), channel_id=1, source_target_pairs={{0,192},{64,0},{128,64},{192,128},{1,193},{65,1},{129,65},{193,129... | collective-permute-start | bytes 1572872 | tf_op jit(solution)/shard_map/ppermute | solution.py:27
  57.5 14.5 %collective-permute-start.1 = (f32[128,1024]{1,0:T(8,128)}, f32[128,1024]{1,0:T(8,128)}, u32[]{:S(2)}, u32[]{:S(2)}) collective-permute-start(f32[128,1024]{1,0:T(8,128)} %get-tuple-element.16), channel_id=1, source_target_pairs={{0,128},{64,192},{128,0},{192,64},{1,129},{65,193},{129,1},{193,65... | collective-permute-start | bytes 1572872 | tf_op jit(solution)/shard_map/ppermute | solution.py:27
  58.8 25.6 %collective-permute-start = (f32[128,1024]{1,0:T(8,128)S(1)}, f32[128,1024]{1,0:T(8,128)}, u32[]{:S(2)}, u32[]{:S(2)}) collective-permute-start(f32[128,1024]{1,0:T(8,128)S(1)} %get-tuple-element.14), channel_id=1, source_target_pairs={{0,64},{64,128},{128,192},{192,0},{1,65},{65,129},{129,193},{193,1... | collective-permute-start | bytes 1572872 | tf_op jit(solution)/shard_map/ppermute | solution.py:27
  206.7 3.6 copy-start.4
  206.7 3.6 copy-start.6
  224.4 6.7 %copy-start.5 = (bf16[2048,64]{0,1:T(8,128)(2,1)S(1)}, bf16[2048,64]{0,1:T(8,128)(2,1)}, u32[]{:S(2)}) copy-start(bf16[2048,64]{0,1:T(8,128)(2,1)} %param.13) | copy-start | bytes 786436
  224.4 147.3 %all-to-all-start.3 = ((bf16[64,24,2048]{2,1,0:T(8,128)(2,1)}), bf16[64,24,2048]{2,1,0:T(8,128)(2,1)}, u32[]{:S(2)}, u32[]{:S(2)}) async-start(bf16[64,24,2048]{2,1,0:T(8,128)(2,1)} %bitcast.60), calls=%async_computation.3 | async-start | bytes 12582912 | tf_op jit(solution)/shard_map/all_to_all | solution.py:100
  375.6 4.0 copy-start.3

commit v5 on v4

--- a/solution.py
+++ b/solution.py
@@ -48,31 +48,30 @@
     placed = (member.T[:, None, :] > 0) & (row_ranks.T[:, None, :] == slot_pos[None, :, None])
     dispatch = placed.reshape(slots, tok_rows).astype(jnp.bfloat16)
 
-    half = feat_width // 2
+    first = feat_width // 4
+    bounds = [(0, first), (first, feat_width)]
     flat_heads = attn_heads.reshape(groups * tok_rows, quarter)
     partials = [
-        jnp.dot(flat_heads, w_out[:, c * half : (c + 1) * half], preferred_element_type=jnp.float32)
-        for c in range(2)
+        jnp.dot(flat_heads, w_out[:, lo:hi], preferred_element_type=jnp.float32) for lo, hi in bounds
     ]
     pieces = lax.all_to_all(
-        partials[0].reshape(groups, tok_rows, half), "dp", split_axis=0, concat_axis=0, tiled=True
+        partials[0].reshape(groups, tok_rows, first), "dp", split_axis=0, concat_axis=0, tiled=True
     )
     part = jnp.sum(pieces, axis=0)
     mid_parts = []
     arrived_parts = []
-    for c in range(2):
-        cols = slice(c * half, (c + 1) * half)
-        res_c, part = lax.optimization_barrier((residual[:, cols], part))
+    for c, (lo, hi) in enumerate(bounds):
+        res_c, part = lax.optimization_barrier((residual[:, lo:hi], part))
         mid_c = (res_c.astype(jnp.float32) + part).astype(jnp.bfloat16)
         mid_parts.append(mid_c)
         outgoing = jnp.dot(dispatch, mid_c, preferred_element_type=jnp.float32).astype(jnp.bfloat16)
         if c == 0:
             outgoing, following = lax.optimization_barrier((outgoing, partials[1]))
-            part = dp_reduce(following.reshape(groups, tok_rows, half))
+            part = dp_reduce(following.reshape(groups, tok_rows, feat_width - first))
         arrived_parts.append(
             lax.all_to_all(
-                outgoing.reshape(experts, capacity, half), "tp", split_axis=0, concat_axis=0, tiled=True
-            ).reshape(slots, half)
+                outgoing.reshape(experts, capacity, hi - lo), "tp", split_axis=0, concat_axis=0, tiled=True
+            ).reshape(slots, hi - lo)
         )
     mid_wide = jnp.concatenate(mid_parts, axis=1).astype(jnp.float32)
     normed = rms_scale(mid_wide, moe_gain).astype(jnp.bfloat16)

time: 412 us -> 409 us (level)
  blocking collectives: 108 us -> 146 us
  waiting for transfers between devices: 223 us -> 185 us
    all_to_all x2, waiting for transfers between devices: 57.4 us -> 8 us  [the longest x1 8 us: local(): lax.all_to_all(partials[0].reshape(groups, tok_rows, first), 'dp', split_...]
    all_to_all x1, blocking collectives: 79.2 us -> 118 us  [local(): lax.all_to_all(outgoing.reshape(experts, capacity, hi - lo), 'tp', split_...]
    ppermute x3, waiting for transfers between devices: 25.6 us -> 36.9 us  [dp_reduce(): total = total + lax.ppermute(sent, 'dp', pairs)]
  transfers between devices with their start and end apart: 6 -> 6, of which waited for: 6 -> 5; matrix products, arithmetic and copies ran while one was open for 3% -> 4% of each run, Pallas kernels for 0% -> 0%
where the time goes in v5:
time: 409 us; the launch traced here: 408 us
  waiting for transfers between devices  185 us (45%)
  blocking collectives  146 us (36%)
  matrix products  34 us (8%)
  starting transfers between devices  27.8 us (7%)
  other arithmetic  9.47 us (2%)
  local copies, waits for them, and re-layouts  4.85 us (1%)
    all_to_all x1, waiting for transfers between devices, local(): lax.all_to_all(served.reshape(experts, capacity, feat_width), 'tp', split...  140 us
    all_to_all x1, blocking collectives, local(): lax.all_to_all(outgoing.reshape(experts, capacity, hi - lo), 'tp', split_...  118 us
    ppermute x3, waiting for transfers between devices, dp_reduce(): total = total + lax.ppermute(sent, 'dp', pairs)  36.9 us
    all_to_all x1, blocking collectives, local(): lax.all_to_all(copies, 'dp', split_axis=0, concat_axis=0, tiled=True)  28.6 us
    all_to_all x1, starting transfers between devices, local(): lax.all_to_all(outgoing.reshape(experts, capacity, hi - lo), 'tp', split_...  14.2 us
    dot_general x1, matrix products, local(): projected_up = jnp.dot(arrived, gate_up, preferred_element_type=jnp.float32)  8.22 us
  transfers between devices with their start and end apart: 6, of which 5 were waited for; matrix products, arithmetic and copies ran while one was open for 4% of the time, Pallas kernels for 0%

profile of v5, /device:TPU:1, one launch (start us, length us, event | category | flops | bytes accessed | tf_op | source)
XLA Modules:
  0.0 408.4 jit_solution(5234209719861650449)
XLA Ops:
  0.6 0.0 copy-start
  0.6 2.8 fusion.26
  3.4 5.0 %all-to-all-start = ((f32[4,128,512]{2,1,0:T(8,128)}), f32[4,128,512]{2,1,0:T(8,128)S(1)}, u32[]{:S(2)}, u32[]{:S(2)}) async-start(f32[4,128,512]{2,1,0:T(8,128)} %fusion.26), calls=%async_computation | async-start | bytes 2097152 | tf_op jit(solution)/shard_map/all_to_all | solution.py:57
  8.4 0.1 eq.50
  8.5 0.7 convert_reduce_fusion
  9.2 0.1 convolution_convert_fusion.3
  9.4 0.3 fusion.23
  9.7 4.2 %fusion.14 = f32[512,1536]{1,0:T(8,128)} fusion(bf16[512,512]{1,0:T(8,128)(2,1)} %bitcast.61, bf16[512,2048]{1,0:T(8,128)(2,1)} %param.10), kind=kOutput, calls=%fused_computation.23 | convolution fusion | flops 805306368 | bytes 5242880 | tf_op jit(solution)/shard_map/dot_general | solution.py:55
  13.9 8.0 %all-to-all-done = f32[4,128,512]{2,1,0:T(8,128)S(1)} async-done(((f32[4,128,512]{2,1,0:T(8,128)}), f32[4,128,512]{2,1,0:T(8,128)S(1)}, u32[]{:S(2)}, u32[]{:S(2)}) %all-to-all-start) | async-done | bytes 1048608 | tf_op jit(solution)/shard_map/all_to_all | solution.py:57
  21.9 0.8 reduce_sum.72
  22.7 0.0 slice-done
  22.7 1.0 add_convert_fusion.1
  23.7 1.7 convolution_convert_fusion.2
  25.4 14.2 %all-to-all-start.1 = ((bf16[64,24,512]{2,1,0:T(8,128)(2,1)}), bf16[64,24,512]{2,1,0:T(8,128)(2,1)}, u32[]{:S(2)}, u32[]{:S(2)}) async-start(bf16[64,24,512]{2,1,0:T(8,128)(2,1)} %bitcast.60), calls=%async_computation.1 | async-start | bytes 3145728 | tf_op jit(solution)/shard_map/all_to_all | solution.py:72
  39.6 0.0 slice-start.1
  39.6 3.2 dynamic-slice_bitcast_fusion.2
  42.8 0.9 collective-permute-start.2
  43.7 1.2 collective-permute-start.1
  44.9 0.0 collective-permute-start
  44.9 16.8 %collective-permute-done.2 = f32[128,1536]{1,0:T(8,128)} collective-permute-done((f32[128,1536]{1,0:T(8,128)}, f32[128,1536]{1,0:T(8,128)}, u32[]{:S(2)}, u32[]{:S(2)}) %collective-permute-start.2) | collective-permute-done | bytes 786464 | tf_op jit(solution)/shard_map/ppermute | solution.py:27
  61.7 2.2 collective-permute-done.1
  63.8 18.0 %collective-permute-done = f32[128,1536]{1,0:T(8,128)} collective-permute-done((f32[128,1536]{1,0:T(8,128)}, f32[128,1536]{1,0:T(8,128)}, u32[]{:S(2)}, u32[]{:S(2)}) %collective-permute-start) | collective-permute-done | bytes 786464 | tf_op jit(solution)/shard_map/ppermute | solution.py:27
  81.8 2.1 fusion.21
  83.9 0.0 slice-done.1
  83.9 0.1 add_convert_fusion
  84.0 3.5 convolution_convert_fusion.1
  87.5 0.0 all-to-all-done.1
  87.5 117.6 %all_to_all.25 = bf16[64,24,1536]{2,1,0:T(8,128)(2,1)S(1)} all-to-all(bf16[64,24,1536]{2,1,0:T(8,128)(2,1)} %bitcast.54), channel_id=1, replica_groups=mesh['dp'=4,'tp'=64] {'tp'}, dimensions={0} | all-to-all | bytes 9437184 | tf_op jit(solution)/shard_map/all_to_all | solution.py:72
  205.1 3.2 fusion
  208.3 0.0 copy-done.3
  208.3 0.0 copy-done.5
  208.3 8.2 %fusion.3 = f32[1536,1024]{1,0:T(8,128)S(1)} fusion(f32[2048]{0:T(1024)S(1)} %copy-done.5, f32[1536]{0:T(1024)S(1)} %add_rsqrt_fusion, bf16[1,2048,1024]{2,1,0:T(8,128)(2,1)S(1)} %copy-done.3, bf16[1536,1536]{1,0:T(8,128)(2,1)S(1)} %bitcast.58, bf16[1536,512]{1,0:T(8,128)(2,1)} %bitcast.12), kind=kOutput, calls=%fused_computation.7 | convolution fusion | flops 6464471040 | bytes 16791552 | tf_op jit(solution)/shard_map/dot_general | solution.py:93
  216.5 0.0 copy-done
  216.6 5.3 %convolution_convert_fusion = bf16[1536,2048]{1,0:T(8,128)(2,1)} fusion(bf16[1,512,2048]{2,1,0:T(8,128)(2,1)S(1)} %copy-done, f32[1536,1024]{1,0:T(8,128)S(1)} %fusion.3), kind=kOutput, calls=%fused_computation.5 | convolution fusion | flops 3229089792 | bytes 14680064 | tf_op jit(solution)/shard_map/dot_general | solution.py:97
  221.9 6.6 %all-to-all-start.3 = ((bf16[64,24,2048]{2,1,0:T(8,128)(2,1)}), bf16[64,24,2048]{2,1,0:T(8,128)(2,1)}, u32[]{:S(2)}, u32[]{:S(2)}) async-start(bf16[64,24,2048]{2,1,0:T(8,128)(2,1)} %bitcast.59), calls=%async_computation.3 | async-start | bytes 12582912 | tf_op jit(solution)/shard_map/all_to_all | solution.py:99
  228.5 0.2 fusion.16
  228.7 0.0 copy-done.4
  228.7 0.4 fusion.24
  229.0 0.0 copy-done.1
  229.2 140.1 %all-to-all-done.3 = bf16[64,24,2048]{2,1,0:T(8,128)(2,1)} async-done(((bf16[64,24,2048]{2,1,0:T(8,128)(2,1)}), bf16[64,24,2048]{2,1,0:T(8,128)(2,1)}, u32[]{:S(2)}, u32[]{:S(2)}) %all-to-all-start.3) | async-done | bytes 6291488 | tf_op jit(solution)/shard_map/all_to_all | solution.py:99
  369.3 3.8 convolution_bitcast_fusion
  373.1 0.0 copy-start.2
  373.1 3.9 multiply_reduce_fusion
  377.1 0.0 copy-done.2
  377.1 1.0 multiply_convert_fusion
  378.1 0.2 broadcast_in_dim.41
  378.4 28.6 %all_to_all.26 = bf16[4,128,2048]{2,1,0:T(8,128)(2,1)S(1)} all-to-all(bf16[4,128,2048]{2,1,0:T(8,128)(2,1)S(1)} %broadcast_in_dim.41), channel_id=1, replica_groups=mesh['dp'=4,'tp'=64] {'dp'}, dimensions={0} | all-to-all | bytes 4194304 | tf_op jit(solution)/shard_map/all_to_all | solution.py:111
  407.0 1.3 copy.25
  (14 shorter events, 0.1 us)
Async XLA Ops:
  0.6 215.9 %copy-start = (bf16[1,512,2048]{2,1,0:T(8,128)(2,1)S(1)}, bf16[1,512,2048]{2,1,0:T(8,128)(2,1)}, u32[]{:S(2)}) copy-start(bf16[1,512,2048]{2,1,0:T(8,128)(2,1)} %param.16) | copy-start | bytes 6291460
  3.4 18.5 %all-to-all-start = ((f32[4,128,512]{2,1,0:T(8,128)}), f32[4,128,512]{2,1,0:T(8,128)S(1)}, u32[]{:S(2)}, u32[]{:S(2)}) async-start(f32[4,128,512]{2,1,0:T(8,128)} %fusion.26), calls=%async_computation | async-start | bytes 2097152 | tf_op jit(solution)/shard_map/all_to_all | solution.py:57
  8.4 14.3 %slice-start = ((bf16[128,2048]{1,0:T(8,128)(2,1)}), bf16[128,512]{1,0:T(8,128)(2,1)S(1)}, s32[]{:S(2)}) async-start(bf16[128,2048]{1,0:T(8,128)(2,1)} %param.11), calls=%async_computation.5 | async-start | bytes 262144 | tf_op jit(solution)/shard_map/slice | solution.py:64
  25.4 62.1 %all-to-all-start.1 = ((bf16[64,24,512]{2,1,0:T(8,128)(2,1)}), bf16[64,24,512]{2,1,0:T(8,128)(2,1)}, u32[]{:S(2)}, u32[]{:S(2)}) async-start(bf16[64,24,512]{2,1,0:T(8,128)(2,1)} %bitcast.60), calls=%async_computation.1 | async-start | bytes 3145728 | tf_op jit(solution)/shard_map/all_to_all | solution.py:72
  39.6 44.3 %slice-start.1 = ((bf16[128,2048]{1,0:T(8,128)(2,1)}), bf16[128,1536]{1,0:T(8,128)(2,1)S(1)}, s32[]{:S(2)}) async-start(bf16[128,2048]{1,0:T(8,128)(2,1)} %param.11), calls=%async_computation.6 | async-start | bytes 786432 | tf_op jit(solution)/shard_map/slice | solution.py:64
  42.8 18.9 %collective-permute-start.2 = (f32[128,1536]{1,0:T(8,128)}, f32[128,1536]{1,0:T(8,128)}, u32[]{:S(2)}, u32[]{:S(2)}) collective-permute-start(f32[128,1536]{1,0:T(8,128)} %get-tuple-element.15), channel_id=1, source_target_pairs={{0,192},{64,0},{128,64},{192,128},{1,193},{65,1},{129,65},{193,129... | collective-permute-start | bytes 2359304 | tf_op jit(solution)/shard_map/ppermute | solution.py:27
  43.7 20.2 %collective-permute-start.1 = (f32[128,1536]{1,0:T(8,128)}, f32[128,1536]{1,0:T(8,128)}, u32[]{:S(2)}, u32[]{:S(2)}) collective-permute-start(f32[128,1536]{1,0:T(8,128)} %get-tuple-element.16), channel_id=1, source_target_pairs={{0,128},{64,192},{128,0},{192,64},{1,129},{65,193},{129,1},{193,65... | collective-permute-start | bytes 2359304 | tf_op jit(solution)/shard_map/ppermute | solution.py:27
  44.9 37.0 %collective-permute-start = (f32[128,1536]{1,0:T(8,128)}, f32[128,1536]{1,0:T(8,128)}, u32[]{:S(2)}, u32[]{:S(2)}) collective-permute-start(f32[128,1536]{1,0:T(8,128)} %get-tuple-element.14), channel_id=1, source_target_pairs={{0,64},{64,128},{128,192},{192,0},{1,65},{65,129},{129,193},{193,1... | collective-permute-start | bytes 2359304 | tf_op jit(solution)/shard_map/ppermute | solution.py:27
  205.1 3.2 copy-start.3
  205.1 3.2 copy-start.5
  221.9 6.8 %copy-start.4 = (bf16[2048,64]{0,1:T(8,128)(2,1)S(1)}, bf16[2048,64]{0,1:T(8,128)(2,1)}, u32[]{:S(2)}) copy-start(bf16[2048,64]{0,1:T(8,128)(2,1)} %param.13) | copy-start | bytes 786436
  221.9 7.2 %copy-start.1 = (s32[128,8]{0,1:T(8,128)S(1)}, s32[128,8]{0,1:T(8,128)}, u32[]{:S(2)}) copy-start(s32[128,8]{0,1:T(8,128)} %param.14) | copy-start | bytes 12292
  221.9 147.4 %all-to-all-start.3 = ((bf16[64,24,2048]{2,1,0:T(8,128)(2,1)}), bf16[64,24,2048]{2,1,0:T(8,128)(2,1)}, u32[]{:S(2)}, u32[]{:S(2)}) async-start(bf16[64,24,2048]{2,1,0:T(8,128)(2,1)} %bitcast.59), calls=%async_computation.3 | async-start | bytes 12582912 | tf_op jit(solution)/shard_map/all_to_all | solution.py:99
  373.1 4.0 copy-start.2
